TPU v7x, 256 devices: a whole 4x4x8 slice. The times are simulated.
256 devices in a mesh: section: 16 (over x, z_lo, core), dp: 16 (over z_hi, y).
Axes of the slice: x: 4, y: 4, z: 8 (z_hi: 4, z_lo: 2; z = z_hi * 2 + z_lo), core: 2. Of those that a mesh axis runs over, the one named last changes fastest.
Arguments:
- encoder_out: bfloat16 [2, 2, 256, 4096], P(None, None, 'dp', 'section'), may hold values from -6 to 6
- encoder_len: int32 [2, 2], replicated, may hold values from 1 to 2, as said below
- decoder_len: int32 [2, 2], replicated, may hold values from 1 to 2, as said below
- queries: bfloat16 [16, 2, 2, 256, 4096], P('section', None, None, None, 'dp'), may hold values from -40 to 40
- cotangent: bfloat16 [16, 2, 2, 256, 4096], P('section', None, None, None, 'dp'), may hold values from -6 to 6
- key_weight: bfloat16 [16, 4096, 4096], P('section', None, 'dp'), may hold values from -0.09375 to 0.09375
- value_weight: bfloat16 [16, 4096, 4096], P('section', None, 'dp'), may hold values from -0.09375 to 0.09375
Outputs:
- attention: bfloat16 [16, 2, 2, 256, 4096], P('section', None, None, None, 'dp')
- grad_query: bfloat16 [16, 2, 2, 256, 4096], P('section', None, None, None, 'dp')
- grad_key_weight: bfloat16 [16, 4096, 4096], P('section', None, 'dp')
- grad_value_weight: bfloat16 [16, 4096, 4096], P('section', None, 'dp')
- grad_encoder: float32 [2, 2, 256, 4096], P(None, None, 'dp', 'section')
Inputs may be any that keep to these rules, and one draw needn't show every extreme that they name: `encoder_len`: in every micro-batch some example fills all 2 encoder blocks. `decoder_len`: in every micro-batch some example fills all 2 decoder blocks.
All inputs are finite; a program needn't handle non-finite values.
Results may differ from a plain program's by a relative error of at most 0.012.
The roundings to bfloat16 on the way count: a program that leaves them out, or rounds other values in their place, can miss the bound.
Values may be sent and summed in bfloat16 or wider, within the bound.
No kernel may reach another device: no remote copies, remote signals or barrier semaphores. Data moves between devices by JAX's collectives and lax.ppermute only.
A program may use at most 128 MiB of HBM per device.

v0:
```python
import jax
import jax.numpy as jnp
from jax import lax
from jax.sharding import PartitionSpec as P

HD = 256
BLOCK = 128
ENC_BLOCKS = 2
MICRO = 2


NEG_FILL = -1e30


def attend(query_rows, key_rows, value_rows, cotan_rows, key_valid, query_valid):
    score_scale = HD ** (-0.5)
    scores = (
        jnp.einsum("eqhd,ekhd->ehqk", query_rows, key_rows, preferred_element_type=jnp.float32)
        * score_scale
    )
    scores = jnp.where(key_valid[:, None, None, :], scores, NEG_FILL)
    largest = jnp.max(scores, axis=-1, keepdims=True)
    weights = jnp.exp(scores - largest)
    probs = weights / jnp.sum(weights, axis=-1, keepdims=True)
    probs_low = probs.astype(jnp.bfloat16)
    attended = jnp.einsum(
        "ehqk,ekhd->eqhd", probs_low, value_rows, preferred_element_type=jnp.float32
    )
    attended = jnp.where(query_valid[:, :, None, None], attended, 0.0).astype(jnp.bfloat16)
    cotan_kept = jnp.where(query_valid[:, :, None, None], cotan_rows, jnp.zeros_like(cotan_rows))
    grad_value = jnp.einsum(
        "ehqk,eqhd->ekhd", probs_low, cotan_kept, preferred_element_type=jnp.float32
    ).astype(jnp.bfloat16)
    grad_probs = jnp.einsum(
        "eqhd,ekhd->ehqk", cotan_kept, value_rows, preferred_element_type=jnp.float32
    )
    inner_sum = jnp.sum(probs * grad_probs, axis=-1, keepdims=True)
    grad_scores = (probs * (grad_probs - inner_sum) * score_scale).astype(jnp.bfloat16)
    grad_query = jnp.einsum(
        "ehqk,ekhd->eqhd", grad_scores, key_rows, preferred_element_type=jnp.float32
    ).astype(jnp.bfloat16)
    grad_key = jnp.einsum(
        "ehqk,eqhd->ekhd", grad_scores, query_rows, preferred_element_type=jnp.float32
    ).astype(jnp.bfloat16)
    return (attended, grad_query, grad_key, grad_value)


def body(encoder_out, encoder_len, decoder_len, queries, cotangent, key_weight, value_weight):
    key_mat = key_weight[0]
    value_mat = value_weight[0]
    width_dev = key_mat.shape[1]
    heads_dev = width_dev // HD
    enc_rows = ENC_BLOCKS * BLOCK
    dec_rows = queries.shape[3]
    examples = queries.shape[2]
    rows_dev = enc_rows // lax.axis_size("dp")
    key_positions = jnp.arange(enc_rows, dtype=jnp.int32)
    query_positions = jnp.arange(dec_rows, dtype=jnp.int32)
    key_acc = jnp.zeros(key_mat.shape, jnp.float32)
    value_acc = jnp.zeros(value_mat.shape, jnp.float32)
    attn_list, query_list, encoder_list = ([], [], [])
    for micro_idx in range(MICRO):
        local_enc = encoder_out[micro_idx]
        wide_enc = lax.all_gather(local_enc, "section", axis=2, tiled=True)
        whole_enc = lax.all_gather(wide_enc, "dp", axis=1, tiled=True)
        key_rows = jnp.einsum(
            "ekd,dc->ekc", whole_enc, key_mat, preferred_element_type=jnp.float32
        ).astype(jnp.bfloat16)
        value_rows = jnp.einsum(
            "ekd,dc->ekc", whole_enc, value_mat, preferred_element_type=jnp.float32
        ).astype(jnp.bfloat16)
        key_valid = key_positions[None, :] < (BLOCK * encoder_len[micro_idx])[:, None]
        query_valid = query_positions[None, :] < (BLOCK * decoder_len[micro_idx])[:, None]
        attended, grad_query, grad_key, grad_value = attend(
            queries[0, micro_idx].reshape(examples, dec_rows, heads_dev, HD),
            key_rows.reshape(examples, enc_rows, heads_dev, HD),
            value_rows.reshape(examples, enc_rows, heads_dev, HD),
            cotangent[0, micro_idx].reshape(examples, dec_rows, heads_dev, HD),
            key_valid,
            query_valid,
        )
        key_flat = grad_key.reshape(examples, enc_rows, width_dev)
        value_flat = grad_value.reshape(examples, enc_rows, width_dev)
        key_acc = key_acc + jnp.einsum(
            "ekd,ekc->dc", whole_enc, key_flat, preferred_element_type=jnp.float32
        )
        value_acc = value_acc + jnp.einsum(
            "ekd,ekc->dc", whole_enc, value_flat, preferred_element_type=jnp.float32
        )

        def head_term(first_row, row_count, key_flat=key_flat, value_flat=value_flat):
            return jnp.einsum(
                "ekc,dc->ked", key_flat, key_mat, preferred_element_type=jnp.float32
            ) + jnp.einsum("ekc,dc->ked", value_flat, value_mat, preferred_element_type=jnp.float32)

        head_share = lax.psum_scatter(
            head_term(jnp.int32(0), lax.axis_size("dp") * rows_dev),
            "dp",
            scatter_dimension=0,
            tiled=True,
        )
        section_share = lax.psum_scatter(head_share, "section", scatter_dimension=2, tiled=True)
        encoder_list.append(jnp.transpose(section_share, (1, 0, 2)))
        attn_list.append(attended.reshape(examples, dec_rows, width_dev))
        query_list.append(grad_query.reshape(examples, dec_rows, width_dev))
    attention = jnp.stack(attn_list)[None]
    query_grads = jnp.stack(query_list)[None]
    key_grads = key_acc.astype(jnp.bfloat16)[None]
    value_grads = value_acc.astype(jnp.bfloat16)[None]
    return (attention, query_grads, key_grads, value_grads, jnp.stack(encoder_list))


def solution(mesh):
    placed = (
        P(None, None, "dp", "section"),
        P(),
        P(),
        P("section", None, None, None, "dp"),
        P("section", None, None, None, "dp"),
        P("section", None, "dp"),
        P("section", None, "dp"),
    )
    return jax.shard_map(
        body,
        mesh=mesh,
        in_specs=placed,
        out_specs=(
            P("section", None, None, None, "dp"),
            P("section", None, None, None, "dp"),
            P("section", None, "dp"),
            P("section", None, "dp"),
            P(None, None, "dp", "section"),
        ),
        check_vma=False,
    )
```

profile of v0, /device:TPU:32, one launch (start us, length us, event | category | flops | bytes accessed | tf_op | source)
XLA Modules:
  0.0 564.6 jit_solution(17353738464398229318)
XLA Ops:
  8.1 20.0 %all-gather = bf16[1,2,16,4096]{3,2,1,0:T(8,128)(2,1)} all-gather(bf16[1,2,16,256]{3,2,1,0:T(8,128)(2,1)S(1)} %get-tuple-element.10), channel_id=2, replica_groups=mesh['section'=16,'dp'=16] {'section'}, dimensions={3}, use_global_device_ids=true | all-gather | bytes 278528 | tf_op jit(solution)/shard_map/all_gather | solution.py:64
  28.2 21.2 %all-gather.2 = bf16[1,2,16,4096]{3,2,1,0:T(8,128)(2,1)} all-gather(bf16[1,2,16,256]{3,2,1,0:T(8,128)(2,1)S(1)} %get-tuple-element.11), channel_id=4, replica_groups=mesh['section'=16,'dp'=16] {'section'}, dimensions={3}, use_global_device_ids=true | all-gather | bytes 278528 | tf_op jit(solution)/shard_map/all_gather | solution.py:64
  51.1 56.0 %all-gather.7.cloned.1.call-done = bf16[1,2,256,4096]{3,2,1,0:T(8,128)(2,1)} async-done(((bf16[1,2,16,4096]{3,2,1,0:T(8,128)(2,1)}), bf16[1,2,256,4096]{3,2,1,0:T(8,128)(2,1)}) %all-gather.7.cloned.1.call-update) | async-done | bytes 4194320 | tf_op jit(solution)/shard_map/all_gather | solution.py:65
  107.1 4.2 fusion.48
  111.8 2.0 fusion.53
  113.7 2.1 fusion.144
  115.8 1.7 convolution_convert_fusion.3
  117.6 1.8 fusion.74
  119.4 1.3 fusion.24
  121.0 4.6 add_bitcast_fusion.1
  125.9 59.0 %all-gather.9.cloned.1.call-done = bf16[1,2,256,4096]{3,2,1,0:T(8,128)(2,1)} async-done(((bf16[1,2,16,4096]{3,2,1,0:T(8,128)(2,1)}), bf16[1,2,256,4096]{3,2,1,0:T(8,128)(2,1)}) %all-gather.9.cloned.1.call-update) | async-done | bytes 4194320 | tf_op jit(solution)/shard_map/all_gather | solution.py:65
  185.0 4.2 fusion.58
  189.2 2.2 fusion.99
  192.7 2.2 fusion.141
  194.9 1.9 convolution_convert_fusion.2
  196.8 1.8 fusion.75
  200.5 4.6 add_bitcast_fusion
  206.3 1.3 fusion.76
  207.6 1.3 fusion.77
  208.9 98.4 %reduce-scatter.5.cloned.1.call-done = f32[16,2,4096]{2,0,1:T(8,128)} async-done(((f32[256,2,4096]{2,0,1:T(8,128)}), f32[16,2,4096]{2,0,1:T(8,128)}) %reduce-scatter.5.cloned.1.call-update) | async-done | bytes 524304 | tf_op jit(solution)/shard_map/reduce_scatter | solution.py:96
  307.6 2.6 fusion.73
  310.2 2.6 fusion.72
  312.8 3.6 convolution_bitcast_fusion.2
  316.5 1.3 fusion.8
  317.8 112.4 %reduce-scatter.9.cloned.1.call-done = f32[16,2,4096]{2,0,1:T(8,128)} async-done(((f32[256,2,4096]{2,0,1:T(8,128)}), f32[16,2,4096]{2,0,1:T(8,128)}) %reduce-scatter.9.cloned.1.call-update) | async-done | bytes 524304 | tf_op jit(solution)/shard_map/reduce_scatter | solution.py:96
  434.3 2.4 copy.32
  436.8 3.6 convolution_bitcast_fusion
  440.4 2.6 fusion.9
  443.0 4.1 copy.33
  447.1 44.8 %reduce-scatter.7.cloned.1.call-done = f32[16,2,256]{2,0,1:T(8,128)} async-done(((f32[16,2,4096]{2,0,1:T(8,128)}), f32[16,2,256]{2,0,1:T(8,128)}) %reduce-scatter.7.cloned.1.call-update) | async-done | bytes 32784 | tf_op jit(solution)/shard_map/reduce_scatter | solution.py:102
  491.9 64.4 %reduce-scatter.11.cloned.1.call-done = f32[16,2,256]{2,0,1:T(8,128)} async-done(((f32[16,2,4096]{2,0,1:T(8,128)}), f32[16,2,256]{2,0,1:T(8,128)}) %reduce-scatter.11.cloned.1.call-update) | async-done | bytes 32784 | tf_op jit(solution)/shard_map/reduce_scatter | solution.py:102
  556.3 1.4 pad_maximum_fusion
  (60 shorter events, 12.4 us)
Async XLA Ops:
  7.2 104.5 %copy-start = (bf16[1,4096,256]{2,1,0:T(8,128)(2,1)S(1)}, bf16[1,4096,256]{2,1,0:T(8,128)(2,1)}, u32[]{:S(2)}) copy-start(bf16[1,4096,256]{2,1,0:T(8,128)(2,1)} %param.12) | copy-start | bytes 6291460
  7.2 99.9 %all-gather.7.cloned.1.call-start = ((), (), s32[]{:S(2)}) async-start(), calls=%async_computation.8 | async-start | bytes 4456448 | tf_op jit(solution)/shard_map/all_gather | solution.py:65
  28.1 156.8 %all-gather.9.cloned.1.call-start = ((), (), s32[]{:S(2)}) async-start(), calls=%async_computation.9 | async-start | bytes 4456448 | tf_op jit(solution)/shard_map/all_gather | solution.py:65
  28.2 83.2 %copy-start.8 = (bf16[1,2,2,256,256]{4,3,2,1,0:T(8,128)(2,1)S(1)}, bf16[1,2,2,256,256]{4,3,2,1,0:T(8,128)(2,1)}, u32[]{:S(2)}) copy-start(bf16[1,2,2,256,256]{4,3,2,1,0:T(8,128)(2,1)} %param.11) | copy-start | bytes 1572868
  49.4 257.9 %reduce-scatter.5.cloned.1.call-start = ((), (), s32[]{:S(2)}) async-start(), calls=%async_computation.4 | async-start | bytes 8912896 | tf_op jit(solution)/shard_map/reduce_scatter | solution.py:96
  107.1 4.6 copy-start.3
  111.7 4.1 copy-start.9
  111.7 2.0 copy-start.13
  119.4 1.7 copy-start.6
  125.7 304.5 %reduce-scatter.9.cloned.1.call-start = ((), (), s32[]{:S(2)}) async-start(), calls=%async_computation.6 | async-start | bytes 8912896 | tf_op jit(solution)/shard_map/reduce_scatter | solution.py:96
  185.0 6.4 %copy-start.2 = (bf16[1,2,256,4096]{3,2,1,0:T(8,128)(2,1)S(1)}, bf16[1,2,256,4096]{3,2,1,0:T(8,128)(2,1)}, u32[]{:S(2)}) copy-start(bf16[1,2,256,4096]{3,2,1,0:T(8,128)(2,1)} %all-gather.9.cloned.1.call-done) | copy-start | bytes 12582916
  189.2 3.5 copy-start.10
  192.7 2.2 copy-start.16
  198.6 1.9 copy-start.7
  205.1 0.9 copy-start.11
  205.1 1.1 copy-start.14
  205.1 1.2 copy-start.17
  205.1 2.5 copy-start.15
  205.2 286.8 %reduce-scatter.7.cloned.1.call-start = ((), (), s32[]{:S(2)}) async-start(), calls=%async_computation.5 | async-start | bytes 557056 | tf_op jit(solution)/shard_map/reduce_scatter | solution.py:102
  307.4 248.9 %reduce-scatter.11.cloned.1.call-start = ((), (), s32[]{:S(2)}) async-start(), calls=%async_computation.7 | async-start | bytes 557056 | tf_op jit(solution)/shard_map/reduce_scatter | solution.py:102
  312.8 3.6 copy-start.4
  316.5 113.8 %copy-start.12 = (bf16[1,2,256,256]{2,3,1,0:T(8,128)(2,1)S(1)}, bf16[1,2,256,256]{2,3,1,0:T(8,128)(2,1)}, u32[]{:S(2)}) copy-start(bf16[1,2,256,256]{2,3,1,0:T(8,128)(2,1)} %fusion.76) | copy-start | bytes 786436
  436.8 3.6 copy-start.5
  440.4 117.3 %copy-start.1 = (bf16[1,4096,256]{2,1,0:T(8,128)(2,1)S(1)}, bf16[1,4096,256]{2,1,0:T(8,128)(2,1)}, u32[]{:S(2)}) copy-start(bf16[1,4096,256]{2,1,0:T(8,128)(2,1)} %param.12) | copy-start | bytes 6291460
Sparse Core Ops, SparseCore 0:
  28.2 78.8 all-gather.6
  109.5 75.3 all-gather.8
  188.7 118.6 reduce-scatter.4
  310.9 119.2 reduce-scatter.8
  432.6 59.3 reduce-scatter.6
  494.3 61.9 reduce-scatter.10
where the time goes:
time: 569 us; the launch traced here: 565 us
  waiting for transfers between devices  435 us (76%)
  matrix products  56.5 us (10%)
  blocking collectives  41.2 us (7%)
  between operations  14.4 us (3%)
  local copies, waits for them, and re-layouts  11.6 us (2%)
    reduce_scatter x2, waiting for transfers between devices, body(): lax.psum_scatter(head_term(jnp.int32(0), lax.axis_size('dp') * rows_dev),...  211 us
    all_gather x2, waiting for transfers between devices, body(): whole_enc = lax.all_gather(wide_enc, 'dp', axis=1, tiled=True)  115 us
    reduce_scatter x2, waiting for transfers between devices, body(): lax.psum_scatter(head_share, 'section', scatter_dimension=2, tiled=True)  109 us
    all_gather x2, blocking collectives, body(): wide_enc = lax.all_gather(local_enc, 'section', axis=2, tiled=True)  41.2 us
  transfers between devices with their start and end apart: 6, of which 6 were waited for; matrix products, arithmetic and copies ran while one was open for 12% of the time, Pallas kernels for 0%

commit v1 on v0

--- a/solution.py
+++ b/solution.py
@@ -59,10 +59,10 @@
     key_acc = jnp.zeros(key_mat.shape, jnp.float32)
     value_acc = jnp.zeros(value_mat.shape, jnp.float32)
     attn_list, query_list, encoder_list = ([], [], [])
+    tall_enc = lax.all_gather(encoder_out, "dp", axis=2, tiled=True)
+    gathered_enc = lax.all_gather(tall_enc, "section", axis=3, tiled=True)
     for micro_idx in range(MICRO):
-        local_enc = encoder_out[micro_idx]
-        wide_enc = lax.all_gather(local_enc, "section", axis=2, tiled=True)
-        whole_enc = lax.all_gather(wide_enc, "dp", axis=1, tiled=True)
+        whole_enc = gathered_enc[micro_idx]
         key_rows = jnp.einsum(
             "ekd,dc->ekc", whole_enc, key_mat, preferred_element_type=jnp.float32
         ).astype(jnp.bfloat16)
@@ -93,21 +93,18 @@
                 "ekc,dc->ked", key_flat, key_mat, preferred_element_type=jnp.float32
             ) + jnp.einsum("ekc,dc->ked", value_flat, value_mat, preferred_element_type=jnp.float32)
 
-        head_share = lax.psum_scatter(
-            head_term(jnp.int32(0), lax.axis_size("dp") * rows_dev),
-            "dp",
-            scatter_dimension=0,
-            tiled=True,
-        )
-        section_share = lax.psum_scatter(head_share, "section", scatter_dimension=2, tiled=True)
-        encoder_list.append(jnp.transpose(section_share, (1, 0, 2)))
+        encoder_list.append(head_term(jnp.int32(0), lax.axis_size("dp") * rows_dev))
         attn_list.append(attended.reshape(examples, dec_rows, width_dev))
         query_list.append(grad_query.reshape(examples, dec_rows, width_dev))
     attention = jnp.stack(attn_list)[None]
     query_grads = jnp.stack(query_list)[None]
     key_grads = key_acc.astype(jnp.bfloat16)[None]
     value_grads = value_acc.astype(jnp.bfloat16)[None]
-    return (attention, query_grads, key_grads, value_grads, jnp.stack(encoder_list))
+    terms = jnp.stack(encoder_list)
+    section_share = lax.psum_scatter(terms, "section", scatter_dimension=3, tiled=True)
+    head_share = lax.psum_scatter(section_share, "dp", scatter_dimension=1, tiled=True)
+    grad_encoder = jnp.transpose(head_share, (0, 2, 1, 3))
+    return (attention, query_grads, key_grads, value_grads, grad_encoder)
 
 
 def solution(mesh):

time: 569 us -> 445 us (0.78)
  waiting for transfers between devices: 435 us -> 300 us
  blocking collectives: 41.2 us -> 52 us
    reduce_scatter x4 -> x2, waiting for transfers between devices: 320 us -> 243 us  [the longest x1 175 us: body(): lax.psum_scatter(terms, 'section', scatter_dimension=3, tiled=True)]
    all_gather x2 -> x1, waiting for transfers between devices: 115 us -> 57.2 us  [body(): gathered_enc = lax.all_gather(tall_enc, 'section', axis=3, tiled=True)]
    all_gather x2 -> x1, blocking collectives: 41.2 us -> 52 us  [body(): tall_enc = lax.all_gather(encoder_out, 'dp', axis=2, tiled=True)]
    dot_general x2, matrix products: 9.27 us -> 2.9 us  [head_term(): jnp.einsum('ekc,dc->ked', value_flat, value_mat, preferred_element_type=j...]
    unnamed x40 -> x30, local copies, waits for them, and re-layouts: 10.7 us -> 12.3 us
  transfers between devices with their start and end apart: 6 -> 3, of which waited for: 6 -> 3; matrix products, arithmetic and copies ran while one was open for 12% -> 7% of each run, Pallas kernels for 0% -> 0%
where the time goes in v1:
time: 445 us; the launch traced here: 443 us
  waiting for transfers between devices  300 us (67%)
  matrix products  56.4 us (13%)
  blocking collectives  52 us (12%)
  between operations  14 us (3%)
  local copies, waits for them, and re-layouts  12.3 us (3%)
  other arithmetic  7.98 us (2%)
    reduce_scatter x1, waiting for transfers between devices, body(): lax.psum_scatter(terms, 'section', scatter_dimension=3, tiled=True)  175 us
    reduce_scatter x1, waiting for transfers between devices, body(): lax.psum_scatter(section_share, 'dp', scatter_dimension=1, tiled=True)  67.8 us
    all_gather x1, waiting for transfers between devices, body(): gathered_enc = lax.all_gather(tall_enc, 'section', axis=3, tiled=True)  57.2 us
    all_gather x1, blocking collectives, body(): tall_enc = lax.all_gather(encoder_out, 'dp', axis=2, tiled=True)  52 us
    unnamed x30, local copies, waits for them, and re-layouts  12.3 us
  transfers between devices with their start and end apart: 3, of which 3 were waited for; matrix products, arithmetic and copies ran while one was open for 7% of the time, Pallas kernels for 0%

profile of v1, /device:TPU:32, one launch (start us, length us, event | category | flops | bytes accessed | tf_op | source)
XLA Modules:
  0.0 443.2 jit_solution(16602837799499248858)
XLA Ops:
  7.2 52.0 %all_gather.6 = bf16[2,2,256,256]{3,2,1,0:T(8,128)(2,1)} all-gather(bf16[2,2,16,256]{3,2,1,0:T(8,128)(2,1)} %param.7), channel_id=1, replica_groups=mesh['section'=16,'dp'=16] {'dp'}, dimensions={2}, use_global_device_ids=true | all-gather | bytes 557056 | tf_op jit(solution)/shard_map/all_gather | solution.py:62
  60.9 57.2 %all-gather.2.cloned.1.call-done = bf16[2,2,256,4096]{3,2,1,0:T(8,128)(2,1)} async-done(((bf16[2,2,256,256]{3,2,1,0:T(8,128)(2,1)}), bf16[2,2,256,4096]{3,2,1,0:T(8,128)(2,1)}) %all-gather.2.cloned.1.call-update) | async-done | bytes 8388624 | tf_op jit(solution)/shard_map/all_gather | solution.py:63
  118.2 4.2 fusion.46
  122.4 1.1 fusion.82
  123.6 1.3 fusion.49
  124.8 2.2 fusion.127
  127.0 1.6 fusion.58
  128.6 4.1 fusion.40
  132.8 1.1 fusion.83
  133.9 3.4 fusion.43
  137.4 2.2 fusion.124
  139.6 1.7 fusion.59
  141.3 1.9 convolution_convert_fusion.3
  143.2 4.5 %fusion.16 = f32[2,256,4096]{2,1,0:T(8,128)} fusion(bf16[2,256,256]{2,1,0:T(8,128)(2,1)S(1)} %convolution_convert_fusion.3, bf16[1,4096,256]{2,1,0:T(8,128)(2,1)S(1)} %copy-done), kind=kOutput, calls=%fused_computation.25 | convolution fusion | flops 1073741824 | bytes 10747904 | tf_op jit(solution)/shard_map/ekc,dc->ked/dot_general | solution.py:92
  147.7 2.0 convolution_convert_fusion.2
  149.8 1.3 fusion.14
  151.1 2.1 copy-done.2
  153.7 1.5 add_bitcast_fusion.1
  155.2 1.4 add_bitcast_fusion
  156.7 6.2 %pad_maximum_fusion = f32[2,256,2,4096]{3,1,2,0:T(8,128)} fusion(f32[1,256,2,4096]{3,1,2,0:T(8,128)S(1)} %add_bitcast_fusion, f32[1,256,2,4096]{3,1,2,0:T(8,128)S(1)} %add_bitcast_fusion.1), kind=kLoop, calls=%fused_computation.4 | loop fusion | flops 4194304 | bytes 33554432 | tf_op jit(solution)/shard_map/stack | solution.py:103
  165.3 1.0 copy.30
  166.3 1.9 fusion.56
  168.2 175.4 %reduce-scatter.3.cloned.1.call-done = f32[2,256,2,256]{3,1,2,0:T(8,128)} async-done(((f32[2,256,2,4096]{3,1,2,0:T(8,128)}), f32[2,256,2,256]{3,1,2,0:T(8,128)}) %reduce-scatter.3.cloned.1.call-update) | async-done | bytes 1048592 | tf_op jit(solution)/shard_map/reduce_scatter | solution.py:104
  343.6 2.0 fusion.57
  345.7 1.0 copy.31
  346.7 3.5 convolution_bitcast_fusion.2
  350.2 3.6 fusion.8
  353.8 2.5 copy.32
  356.3 3.4 convolution_bitcast_fusion
  359.7 5.1 %fusion.9 = bf16[1,4096,256]{1,2,0:T(8,128)(2,1)} fusion(f32[256,4096]{1,0:T(8,128)S(1)} %convolution_bitcast_fusion, bf16[2,256,256]{1,2,0:T(8,128)(2,1)S(1)} %fusion.58, bf16[2,2,256,4096]{3,2,1,0:T(8,128)(2,1)} %all-gather.2.cloned.1.call-done), kind=kOutput, calls=%fused_computation.16 | convolution fusion | flops 1075838976 | bytes 10747904 | tf_op jit(solution)/shard_map/ekd,ekc->dc/dot_general | solution.py:87
  364.8 4.1 copy.33
  368.9 67.8 %reduce-scatter.5.cloned.1.call-done = f32[2,16,2,256]{3,1,2,0:T(8,128)} async-done(((f32[2,256,2,256]{3,1,2,0:T(8,128)}), f32[2,16,2,256]{3,1,2,0:T(8,128)}) %reduce-scatter.5.cloned.1.call-update) | async-done | bytes 65552 | tf_op jit(solution)/shard_map/reduce_scatter | solution.py:105
  (39 shorter events, 4.8 us)
Async XLA Ops:
  7.2 116.4 %copy-start = (bf16[1,4096,256]{2,1,0:T(8,128)(2,1)S(1)}, bf16[1,4096,256]{2,1,0:T(8,128)(2,1)}, u32[]{:S(2)}) copy-start(bf16[1,4096,256]{2,1,0:T(8,128)(2,1)} %param.12) | copy-start | bytes 6291460
  7.2 111.0 %all-gather.2.cloned.1.call-start = ((), (), s32[]{:S(2)}) async-start(), calls=%async_computation.2 | async-start | bytes 8912896 | tf_op jit(solution)/shard_map/all_gather | solution.py:63
  59.2 284.4 %reduce-scatter.3.cloned.1.call-start = ((), (), s32[]{:S(2)}) async-start(), calls=%async_computation.3 | async-start | bytes 17825792 | tf_op jit(solution)/shard_map/reduce_scatter | solution.py:104
  60.9 61.5 %copy-start.5 = (bf16[1,2,2,256,256]{4,3,2,1,0:T(8,128)(2,1)S(1)}, bf16[1,2,2,256,256]{4,3,2,1,0:T(8,128)(2,1)}, u32[]{:S(2)}) copy-start(bf16[1,2,2,256,256]{4,3,2,1,0:T(8,128)(2,1)} %param.11) | copy-start | bytes 1572868
  118.2 5.4 %copy-start.3 = (bf16[2,2,256,4096]{3,2,1,0:T(8,128)(2,1)S(1)}, bf16[2,2,256,4096]{3,2,1,0:T(8,128)(2,1)}, u32[]{:S(2)}) copy-start(bf16[2,2,256,4096]{3,2,1,0:T(8,128)(2,1)} %all-gather.2.cloned.1.call-done) | copy-start | bytes 25165828
  124.8 7.9 %copy-start.11 = (bf16[2,256,256]{2,1,0:T(8,128)(2,1)}, bf16[2,256,256]{2,1,0:T(8,128)(2,1)S(1)}, u32[]{:S(2)}) copy-start(bf16[2,256,256]{2,1,0:T(8,128)(2,1)S(1)} %fusion.49) | copy-start | bytes 786436
  132.8 4.6 %copy-start.6 = (bf16[2,256,256]{2,1,0:T(8,128)(2,1)}, bf16[2,256,256]{2,1,0:T(8,128)(2,1)S(1)}, u32[]{:S(2)}) copy-start(bf16[2,256,256]{2,1,0:T(8,128)(2,1)S(1)} %fusion.40) | copy-start | bytes 786436
  137.4 2.2 copy-start.9
  149.8 3.4 copy-start.2
  149.8 4.0 copy-start.4
  162.9 1.0 copy-start.8
  162.9 1.1 copy-start.12
  162.9 1.7 copy-start.7
  162.9 1.7 copy-start.10
  162.9 273.8 %reduce-scatter.5.cloned.1.call-start = ((), (), s32[]{:S(2)}) async-start(), calls=%async_computation.4 | async-start | bytes 1114112 | tf_op jit(solution)/shard_map/reduce_scatter | solution.py:105
  359.7 77.0 %copy-start.1 = (bf16[1,4096,256]{2,1,0:T(8,128)(2,1)S(1)}, bf16[1,4096,256]{2,1,0:T(8,128)(2,1)}, u32[]{:S(2)}) copy-start(bf16[1,4096,256]{2,1,0:T(8,128)(2,1)} %param.12) | copy-start | bytes 6291460
Sparse Core Ops, SparseCore 0:
  59.3 58.7 all-gather.1
  163.0 180.5 reduce-scatter.2
  347.7 88.9 reduce-scatter.4

commit v2 on v1

--- a/solution.py
+++ b/solution.py
@@ -100,8 +100,9 @@
     query_grads = jnp.stack(query_list)[None]
     key_grads = key_acc.astype(jnp.bfloat16)[None]
     value_grads = value_acc.astype(jnp.bfloat16)[None]
-    terms = jnp.stack(encoder_list)
+    terms = jnp.stack(encoder_list).astype(jnp.bfloat16)
     section_share = lax.psum_scatter(terms, "section", scatter_dimension=3, tiled=True)
+    section_share = section_share.astype(jnp.float32)
     head_share = lax.psum_scatter(section_share, "dp", scatter_dimension=1, tiled=True)
     grad_encoder = jnp.transpose(head_share, (0, 2, 1, 3))
     return (attention, query_grads, key_grads, value_grads, grad_encoder)

time: 445 us -> 365 us (0.82)
  waiting for transfers between devices: 300 us -> 214 us
    reduce_scatter x1, waiting for transfers between devices: 175 us -> 90.6 us  [body(): lax.psum_scatter(terms, 'section', scatter_dimension=3, tiled=True)]
    unnamed x30 -> x46, local copies, waits for them, and re-layouts: 12.3 us -> 13.1 us
  transfers between devices with their start and end apart: 3 -> 3, of which waited for: 3 -> 3; matrix products, arithmetic and copies ran while one was open for 7% -> 9% of each run, Pallas kernels for 0% -> 0%
where the time goes in v2:
time: 365 us; the launch traced here: 363 us
  waiting for transfers between devices  214 us (59%)
  matrix products  60.2 us (16%)
  blocking collectives  52 us (14%)
  between operations  14 us (4%)
  local copies, waits for them, and re-layouts  13.1 us (4%)
  other arithmetic  10.2 us (3%)
    reduce_scatter x1, waiting for transfers between devices, body(): lax.psum_scatter(terms, 'section', scatter_dimension=3, tiled=True)  90.6 us
    reduce_scatter x1, waiting for transfers between devices, body(): lax.psum_scatter(section_share, 'dp', scatter_dimension=1, tiled=True)  65.8 us
    all_gather x1, waiting for transfers between devices, body(): gathered_enc = lax.all_gather(tall_enc, 'section', axis=3, tiled=True)  57.2 us
    all_gather x1, blocking collectives, body(): tall_enc = lax.all_gather(encoder_out, 'dp', axis=2, tiled=True)  52 us
    unnamed x46, local copies, waits for them, and re-layouts  13.1 us
    dot_general x2, matrix products, body(): jnp.einsum('ekd,ekc->dc', whole_enc, value_flat, preferred_element_type=j...  8.61 us
    dot_general x2, matrix products, body(): jnp.einsum('ekd,dc->ekc', whole_enc, value_mat, preferred_element_type=jn...  8.36 us
  transfers between devices with their start and end apart: 3, of which 3 were waited for; matrix products, arithmetic and copies ran while one was open for 9% of the time, Pallas kernels for 0%

profile of v2, /device:TPU:32, one launch (start us, length us, event | category | flops | bytes accessed | tf_op | source)
XLA Modules:
  0.0 363.3 jit_solution(3471289526037257612)
XLA Ops:
  7.2 52.0 %all_gather.6 = bf16[2,2,256,256]{3,2,1,0:T(8,128)(2,1)} all-gather(bf16[2,2,16,256]{3,2,1,0:T(8,128)(2,1)} %param.7), channel_id=1, replica_groups=mesh['section'=16,'dp'=16] {'dp'}, dimensions={2}, use_global_device_ids=true | all-gather | bytes 557056 | tf_op jit(solution)/shard_map/all_gather | solution.py:62
  60.9 57.2 %all-gather.2.cloned.1.call-done = bf16[2,2,256,4096]{3,2,1,0:T(8,128)(2,1)} async-done(((bf16[2,2,256,256]{3,2,1,0:T(8,128)(2,1)}), bf16[2,2,256,4096]{3,2,1,0:T(8,128)(2,1)}) %all-gather.2.cloned.1.call-update) | async-done | bytes 8388624 | tf_op jit(solution)/shard_map/all_gather | solution.py:63
  118.2 4.2 %fusion.48 = bf16[2,256,256]{2,1,0:T(8,128)(2,1)S(1)} fusion(bf16[1,4096,256]{2,1,0:T(8,128)(2,1)} %param.13, bf16[2,2,256,4096]{3,2,1,0:T(8,128)(2,1)} %all-gather.2.cloned.1.call-done), kind=kOutput, calls=%fused_computation.57 | convolution fusion | flops 1073872896 | bytes 6553600 | tf_op jit(solution)/shard_map/ekd,dc->ekc/dot_general | solution.py:69
  122.4 1.1 fusion.84
  123.6 2.0 fusion.51
  125.6 2.1 fusion.129
  127.7 2.3 fusion.60
  130.0 4.1 %fusion.42 = bf16[2,256,256]{2,1,0:T(8,128)(2,1)S(1)} fusion(bf16[1,4096,256]{2,1,0:T(8,128)(2,1)} %param.13, bf16[2,2,256,4096]{3,2,1,0:T(8,128)(2,1)} %all-gather.2.cloned.1.call-done), kind=kOutput, calls=%fused_computation.55 | convolution fusion | flops 1073872896 | bytes 6553600 | tf_op jit(solution)/shard_map/ekd,dc->ekc/dot_general | solution.py:69
  134.1 1.1 fusion.85
  135.2 4.1 %fusion.45 = bf16[2,256,256]{2,1,0:T(8,128)(2,1)} fusion(bf16[1,4096,256]{2,1,0:T(8,128)(2,1)S(1)} %copy-done, bf16[2,2,256,4096]{3,2,1,0:T(8,128)(2,1)} %all-gather.2.cloned.1.call-done), kind=kOutput, calls=%fused_computation.56 | convolution fusion | flops 1073872896 | bytes 6553600 | tf_op jit(solution)/shard_map/ekd,dc->ekc/dot_general | solution.py:66
  139.4 2.1 fusion.126
  141.5 1.7 fusion.61
  143.2 2.1 convolution_convert_fusion.3
  145.3 4.5 %fusion.18 = f32[2,256,4096]{2,1,0:T(8,128)} fusion(bf16[2,256,256]{2,1,0:T(8,128)(2,1)S(1)} %convolution_convert_fusion.3, bf16[1,4096,256]{2,1,0:T(8,128)(2,1)S(1)} %copy-done), kind=kOutput, calls=%fused_computation.27 | convolution fusion | flops 1073741824 | bytes 10747904 | tf_op jit(solution)/shard_map/ekc,dc->ked/dot_general | solution.py:92
  149.8 1.8 convolution_convert_fusion.2
  152.3 1.3 fusion.16
  153.6 2.1 copy-done.2
  156.3 1.3 fusion.4
  157.6 3.3 fusion.5
  160.9 6.3 %pad_maximum_fusion = bf16[2,256,2,4096]{3,1,2,0:T(8,128)(2,1)} fusion(bf16[1,256,2,4096]{3,1,2,0:T(8,128)(2,1)} %fusion.5, bf16[1,256,2,4096]{3,1,2,0:T(8,128)(2,1)S(1)} %fusion.4), kind=kLoop, calls=%fused_computation.4 | loop fusion | flops 4194304 | bytes 16777216 | tf_op jit(solution)/shard_map/stack | solution.py:103
  169.8 1.0 copy.30
  170.8 2.1 fusion.58
  172.8 90.6 %reduce-scatter.3.cloned.1.call-done = bf16[2,256,2,256]{3,1,2,0:T(8,128)(2,1)} async-done(((bf16[2,256,2,4096]{3,1,2,0:T(8,128)(2,1)}), bf16[2,256,2,256]{3,1,2,0:T(8,128)(2,1)}) %reduce-scatter.3.cloned.1.call-update) | async-done | bytes 524304 | tf_op jit(solution)/shard_map/reduce_scatter | solution.py:104
  263.4 2.1 convert_element_type.134
  265.6 1.9 fusion.59
  268.6 3.6 convolution_bitcast_fusion.2
  272.1 3.6 fusion.10
  275.8 2.5 copy.32
  278.2 3.5 convolution_bitcast_fusion
  281.8 5.1 %fusion.11 = bf16[1,4096,256]{1,2,0:T(8,128)(2,1)} fusion(f32[256,4096]{1,0:T(8,128)S(1)} %convolution_bitcast_fusion, bf16[2,256,256]{1,2,0:T(8,128)(2,1)S(1)} %copy-done.6, bf16[2,2,256,4096]{3,2,1,0:T(8,128)(2,1)} %all-gather.2.cloned.1.call-done), kind=kOutput, calls=%fused_computation.18 | convolution fusion | flops 1075838976 | bytes 10747904 | tf_op jit(solution)/shard_map/ekd,ekc->dc/dot_general | solution.py:87
  286.9 4.1 %copy.33 = bf16[1,4096,256]{2,1,0:T(8,128)(2,1)} copy(bf16[1,4096,256]{1,2,0:T(8,128)(2,1)} %fusion.11) | data formatting | bytes 4194304
  290.9 65.8 %reduce-scatter.5.cloned.1.call-done = f32[2,16,2,256]{3,1,2,0:T(8,128)} async-done(((f32[2,256,2,256]{3,1,2,0:T(8,128)}), f32[2,16,2,256]{3,1,2,0:T(8,128)}) %reduce-scatter.5.cloned.1.call-update) | async-done | bytes 65552 | tf_op jit(solution)/shard_map/reduce_scatter | solution.py:106
  (56 shorter events, 6.6 us)
Async XLA Ops:
  7.2 116.4 %copy-start = (bf16[1,4096,256]{2,1,0:T(8,128)(2,1)S(1)}, bf16[1,4096,256]{2,1,0:T(8,128)(2,1)}, u32[]{:S(2)}) copy-start(bf16[1,4096,256]{2,1,0:T(8,128)(2,1)} %param.12) | copy-start | bytes 6291460
  7.2 111.0 %all-gather.2.cloned.1.call-start = ((), (), s32[]{:S(2)}) async-start(), calls=%async_computation.2 | async-start | bytes 8912896 | tf_op jit(solution)/shard_map/all_gather | solution.py:63
  59.2 204.2 %reduce-scatter.3.cloned.1.call-start = ((), (), s32[]{:S(2)}) async-start(), calls=%async_computation.3 | async-start | bytes 8912896 | tf_op jit(solution)/shard_map/reduce_scatter | solution.py:104
  60.9 61.5 %copy-start.11 = (bf16[1,2,2,256,256]{4,3,2,1,0:T(8,128)(2,1)S(1)}, bf16[1,2,2,256,256]{4,3,2,1,0:T(8,128)(2,1)}, u32[]{:S(2)}) copy-start(bf16[1,2,2,256,256]{4,3,2,1,0:T(8,128)(2,1)} %param.11) | copy-start | bytes 1572868
  118.2 5.4 %copy-start.3 = (bf16[2,2,256,4096]{3,2,1,0:T(8,128)(2,1)S(1)}, bf16[2,2,256,4096]{3,2,1,0:T(8,128)(2,1)}, u32[]{:S(2)}) copy-start(bf16[2,2,256,4096]{3,2,1,0:T(8,128)(2,1)} %all-gather.2.cloned.1.call-done) | copy-start | bytes 25165828
  122.4 3.2 copy-start.12
  123.6 2.0 copy-start.16
  134.1 5.3 %copy-start.14 = (bf16[2,256,256]{2,1,0:T(8,128)(2,1)}, bf16[2,256,256]{2,1,0:T(8,128)(2,1)S(1)}, u32[]{:S(2)}) copy-start(bf16[2,256,256]{2,1,0:T(8,128)(2,1)S(1)} %fusion.42) | copy-start | bytes 786436
  145.2 4.5 %copy-start.9 = (bf16[2,256,256]{2,1,0:T(8,128)(2,1)}, bf16[2,256,256]{2,1,0:T(8,128)(2,1)S(1)}, u32[]{:S(2)}) copy-start(bf16[2,256,256]{2,1,0:T(8,128)(2,1)S(1)} %convolution_convert_fusion.3) | copy-start | bytes 786436
  145.2 4.5 %copy-start.17 = (bf16[1,2,2,256,256]{4,3,2,1,0:T(8,128)(2,1)S(1)}, bf16[1,2,2,256,256]{4,3,2,1,0:T(8,128)(2,1)}, u32[]{:S(2)}) copy-start(bf16[1,2,2,256,256]{4,3,2,1,0:T(8,128)(2,1)} %param.10) | copy-start | bytes 1572868
  151.6 0.7 copy-start.7
  152.3 3.4 copy-start.2
  152.3 4.0 %copy-start.4 = (bf16[1,4096,256]{2,1,0:T(8,128)(2,1)S(1)}, bf16[1,4096,256]{2,1,0:T(8,128)(2,1)}, u32[]{:S(2)}) copy-start(bf16[1,4096,256]{2,1,0:T(8,128)(2,1)} %param.13) | copy-start | bytes 6291460
  152.3 4.0 %copy-start.5 = (bf16[2,256,256]{1,2,0:T(8,128)(2,1)S(1)}, bf16[2,256,256]{1,2,0:T(8,128)(2,1)}, u32[]{:S(2)}) copy-start(bf16[2,256,256]{1,2,0:T(8,128)(2,1)} %fusion.60) | copy-start | bytes 786436
  167.3 0.9 copy-start.13
  167.3 1.1 copy-start.18
  167.3 1.2 copy-start.20
  167.3 1.8 copy-start.15
  167.3 1.8 copy-start.19
  167.3 189.4 %reduce-scatter.5.cloned.1.call-start = ((), (), s32[]{:S(2)}) async-start(), calls=%async_computation.4 | async-start | bytes 1114112 | tf_op jit(solution)/shard_map/reduce_scatter | solution.py:106
  172.8 95.7 %copy-start.8 = (bf16[2,256,256]{2,1,0:T(8,128)(2,1)S(1)}, bf16[2,256,256]{2,1,0:T(8,128)(2,1)}, u32[]{:S(2)}) copy-start(bf16[2,256,256]{2,1,0:T(8,128)(2,1)} %copy-done.7) | copy-start | bytes 786436
  268.6 3.6 copy-start.10
  278.2 3.5 copy-start.6
  281.8 75.0 %copy-start.1 = (bf16[1,4096,256]{2,1,0:T(8,128)(2,1)S(1)}, bf16[1,4096,256]{2,1,0:T(8,128)(2,1)}, u32[]{:S(2)}) copy-start(bf16[1,4096,256]{2,1,0:T(8,128)(2,1)} %param.12) | copy-start | bytes 6291460
Sparse Core Ops, SparseCore 0:
  59.3 58.7 all-gather.1
  167.5 95.9 reduce-scatter.2
  267.5 89.1 reduce-scatter.4

commit v3 on v2

--- a/solution.py
+++ b/solution.py
@@ -103,8 +103,13 @@
     terms = jnp.stack(encoder_list).astype(jnp.bfloat16)
     section_share = lax.psum_scatter(terms, "section", scatter_dimension=3, tiled=True)
     section_share = section_share.astype(jnp.float32)
-    head_share = lax.psum_scatter(section_share, "dp", scatter_dimension=1, tiled=True)
-    grad_encoder = jnp.transpose(head_share, (0, 2, 1, 3))
+    micro, enc_rows_all, examples_all, width_sec = section_share.shape
+    groups = lax.axis_size("dp")
+    row_blocks = section_share.reshape(
+        micro, groups, enc_rows_all // groups, examples_all, width_sec
+    ).transpose(1, 0, 3, 2, 4)
+    received = lax.all_to_all(row_blocks, "dp", 0, 0, tiled=True)
+    grad_encoder = jnp.sum(received, axis=0)
     return (attention, query_grads, key_grads, value_grads, grad_encoder)
 
 

time: 365 us -> 315 us (0.86)
  waiting for transfers between devices: 214 us -> 155 us
  starting transfers between devices: 0.12 us -> 10.2 us
    reduce_scatter x1 -> x0, waiting for transfers between devices: 65.8 us -> none  [body(): lax.psum_scatter(section_share, 'dp', scatter_dimension=1, tiled=True)]
    all_to_all x0 -> x1, starting transfers between devices: none -> 10.1 us  [body(): received = lax.all_to_all(row_blocks, 'dp', 0, 0, tiled=True)]
    all_to_all x0 -> x1, waiting for transfers between devices: none -> 8.78 us  [body(): received = lax.all_to_all(row_blocks, 'dp', 0, 0, tiled=True)]
    unnamed x46 -> x50, local copies, waits for them, and re-layouts: 13.1 us -> 13.8 us
  transfers between devices with their start and end apart: 3 -> 3, of which waited for: 3 -> 3; matrix products, arithmetic and copies ran while one was open for 9% -> 10% of each run, Pallas kernels for 0% -> 0%
where the time goes in v3:
time: 315 us; the launch traced here: 314 us
  waiting for transfers between devices  155 us (49%)
  matrix products  57.8 us (18%)
  blocking collectives  52 us (17%)
  between operations  14.4 us (5%)
  local copies, waits for them, and re-layouts  13.8 us (4%)
  other arithmetic  11 us (3%)
  starting transfers between devices  10.2 us (3%)
    reduce_scatter x1, waiting for transfers between devices, body(): lax.psum_scatter(terms, 'section', scatter_dimension=3, tiled=True)  88.7 us
    all_gather x1, waiting for transfers between devices, body(): gathered_enc = lax.all_gather(tall_enc, 'section', axis=3, tiled=True)  57.2 us
    all_gather x1, blocking collectives, body(): tall_enc = lax.all_gather(encoder_out, 'dp', axis=2, tiled=True)  52 us
    unnamed x50, local copies, waits for them, and re-layouts  13.8 us
    all_to_all x1, starting transfers between devices, body(): received = lax.all_to_all(row_blocks, 'dp', 0, 0, tiled=True)  10.1 us
    all_to_all x1, waiting for transfers between devices, body(): received = lax.all_to_all(row_blocks, 'dp', 0, 0, tiled=True)  8.78 us
    dot_general x2, matrix products, body(): jnp.einsum('ekd,ekc->dc', whole_enc, value_flat, preferred_element_type=j...  8.57 us
    dot_general x2, matrix products, body(): jnp.einsum('ekd,dc->ekc', whole_enc, value_mat, preferred_element_type=jn...  8.36 us
  transfers between devices with their start and end apart: 3, of which 3 were waited for; matrix products, arithmetic and copies ran while one was open for 10% of the time, Pallas kernels for 0%

profile of v3, /device:TPU:32, one launch (start us, length us, event | category | flops | bytes accessed | tf_op | source)
XLA Modules:
  0.0 313.8 jit_solution(1010064587376379098)
XLA Ops:
  7.2 52.0 %all_gather.6 = bf16[2,2,256,256]{3,2,1,0:T(8,128)(2,1)} all-gather(bf16[2,2,16,256]{3,2,1,0:T(8,128)(2,1)} %param.7), channel_id=1, replica_groups=mesh['section'=16,'dp'=16] {'dp'}, dimensions={2}, use_global_device_ids=true | all-gather | bytes 557056 | tf_op jit(solution)/shard_map/all_gather | solution.py:62
  60.9 57.2 %all-gather.2.cloned.1.call-done = bf16[2,2,256,4096]{3,2,1,0:T(8,128)(2,1)} async-done(((bf16[2,2,256,256]{3,2,1,0:T(8,128)(2,1)}), bf16[2,2,256,4096]{3,2,1,0:T(8,128)(2,1)}) %all-gather.2.cloned.1.call-update) | async-done | bytes 8388624 | tf_op jit(solution)/shard_map/all_gather | solution.py:63
  118.2 4.2 %fusion.48 = bf16[2,256,256]{2,1,0:T(8,128)(2,1)S(1)} fusion(bf16[1,4096,256]{2,1,0:T(8,128)(2,1)} %param.13, bf16[2,2,256,4096]{3,2,1,0:T(8,128)(2,1)} %all-gather.2.cloned.1.call-done), kind=kOutput, calls=%fused_computation.57 | convolution fusion | flops 1073872896 | bytes 6553600 | tf_op jit(solution)/shard_map/ekd,dc->ekc/dot_general | solution.py:69
  123.4 1.3 fusion.51
  124.7 2.2 fusion.129
  126.9 2.3 fusion.60
  129.2 4.1 %fusion.42 = bf16[2,256,256]{2,1,0:T(8,128)(2,1)S(1)} fusion(bf16[1,4096,256]{2,1,0:T(8,128)(2,1)} %param.13, bf16[2,2,256,4096]{3,2,1,0:T(8,128)(2,1)} %all-gather.2.cloned.1.call-done), kind=kOutput, calls=%fused_computation.55 | convolution fusion | flops 1073872896 | bytes 6553600 | tf_op jit(solution)/shard_map/ekd,dc->ekc/dot_general | solution.py:69
  133.3 1.1 fusion.85
  134.5 3.4 %fusion.45 = bf16[2,256,256]{2,1,0:T(8,128)(2,1)S(1)} fusion(bf16[1,4096,256]{2,1,0:T(8,128)(2,1)S(1)} %copy-done, bf16[2,2,256,4096]{3,2,1,0:T(8,128)(2,1)} %all-gather.2.cloned.1.call-done), kind=kOutput, calls=%fused_computation.56 | convolution fusion | flops 1073872896 | bytes 6553600 | tf_op jit(solution)/shard_map/ekd,dc->ekc/dot_general | solution.py:66
  137.9 2.2 fusion.126
  140.1 1.7 fusion.61
  141.8 1.8 convolution_convert_fusion.3
  143.6 4.5 %fusion.18 = f32[2,256,4096]{2,1,0:T(8,128)} fusion(bf16[2,256,256]{2,1,0:T(8,128)(2,1)S(1)} %convolution_convert_fusion.3, bf16[1,4096,256]{2,1,0:T(8,128)(2,1)S(1)} %copy-done), kind=kOutput, calls=%fused_computation.27 | convolution fusion | flops 1073741824 | bytes 10747904 | tf_op jit(solution)/shard_map/ekc,dc->ked/dot_general | solution.py:92
  148.1 1.8 convolution_convert_fusion.2
  150.7 1.3 fusion.16
  152.0 2.1 copy-done.2
  154.7 1.3 fusion.4
  156.0 3.3 %fusion.5 = bf16[1,256,2,4096]{3,1,2,0:T(8,128)(2,1)} fusion(f32[2,256,4096]{2,1,0:T(8,128)S(1)} %fusion.16, bf16[2,256,256]{1,2,0:T(8,128)(2,1)S(1)} %fusion.61, bf16[1,4096,256]{2,1,0:T(8,128)(2,1)S(1)} %copy-done.4), kind=kOutput, calls=%fused_computation.8 | convolution fusion | flops 1077936128 | bytes 14942208 | tf_op jit(solution)/shard_map/ekc,dc->ked/dot_general | solution.py:94
  159.3 6.3 %pad_maximum_fusion = bf16[2,256,2,4096]{3,1,2,0:T(8,128)(2,1)} fusion(bf16[1,256,2,4096]{3,1,2,0:T(8,128)(2,1)} %fusion.5, bf16[1,256,2,4096]{3,1,2,0:T(8,128)(2,1)S(1)} %fusion.4), kind=kLoop, calls=%fused_computation.4 | loop fusion | flops 4194304 | bytes 16777216 | tf_op jit(solution)/shard_map/stack | solution.py:103
  168.1 1.0 copy.53
  169.1 2.1 fusion.58
  171.2 1.9 fusion.59
  173.1 88.7 %reduce-scatter.2.cloned.1.call-done = bf16[2,256,2,256]{3,1,2,0:T(8,128)(2,1)} async-done(((bf16[2,256,2,4096]{3,1,2,0:T(8,128)(2,1)}), bf16[2,256,2,256]{3,1,2,0:T(8,128)(2,1)}) %reduce-scatter.2.cloned.1.call-update) | async-done | bytes 524304 | tf_op jit(solution)/shard_map/reduce_scatter | solution.py:104
  261.8 2.2 copy_bitcast_fusion
  264.0 10.1 %all-to-all-start = ((f32[16,2,2,16,256]{4,3,2,1,0:T(8,128)}), f32[16,2,2,16,256]{4,3,2,1,0:T(8,128)S(1)}, u32[]{:S(2)}, u32[]{:S(2)}) async-start(f32[16,2,2,16,256]{4,3,2,1,0:T(8,128)} %copy_bitcast_fusion), calls=%async_computation.1 | async-start | bytes 2097152 | tf_op jit(solution)/shard_map/all_to_all | solution.py:111
  275.2 3.6 %convolution_bitcast_fusion.2 = f32[256,4096]{1,0:T(8,128)S(1)} fusion(bf16[2,256,256]{2,1,0:T(8,128)(2,1)S(1)} %copy-done.8, bf16[2,2,256,4096]{3,2,1,0:T(8,128)(2,1)} %all-gather.2.cloned.1.call-done), kind=kOutput, calls=%fused_computation.11 | convolution fusion | flops 1073741824 | bytes 8650752 | tf_op jit(solution)/shard_map/ekd,ekc->dc/dot_general | solution.py:84
  278.8 3.6 %fusion.10 = bf16[1,4096,256]{1,2,0:T(8,128)(2,1)S(1)} fusion(f32[256,4096]{1,0:T(8,128)S(1)} %convolution_bitcast_fusion.2, bf16[2,256,256]{2,1,0:T(8,128)(2,1)S(1)} %copy-done.10, bf16[2,2,256,4096]{3,2,1,0:T(8,128)(2,1)} %all-gather.2.cloned.1.call-done), kind=kOutput, calls=%fused_computation.17 | convolution fusion | flops 1075838976 | bytes 10747904 | tf_op jit(solution)/shard_map/ekd,ekc->dc/dot_general | solution.py:84
  282.4 2.5 copy.55
  284.9 3.5 %convolution_bitcast_fusion = f32[256,4096]{1,0:T(8,128)S(1)} fusion(bf16[2,256,256]{1,2,0:T(8,128)(2,1)S(1)} %fusion.61, bf16[2,2,256,4096]{3,2,1,0:T(8,128)(2,1)} %all-gather.2.cloned.1.call-done), kind=kOutput, calls=%fused_computation.9 | convolution fusion | flops 1073741824 | bytes 8650752 | tf_op jit(solution)/shard_map/ekd,ekc->dc/dot_general | solution.py:87
  288.4 5.1 %fusion.11 = bf16[1,4096,256]{1,2,0:T(8,128)(2,1)} fusion(f32[256,4096]{1,0:T(8,128)S(1)} %convolution_bitcast_fusion, bf16[2,256,256]{1,2,0:T(8,128)(2,1)S(1)} %copy-done.6, bf16[2,2,256,4096]{3,2,1,0:T(8,128)(2,1)} %all-gather.2.cloned.1.call-done), kind=kOutput, calls=%fused_computation.18 | convolution fusion | flops 1075838976 | bytes 10747904 | tf_op jit(solution)/shard_map/ekd,ekc->dc/dot_general | solution.py:87
  293.5 4.1 %copy.56 = bf16[1,4096,256]{2,1,0:T(8,128)(2,1)} copy(bf16[1,4096,256]{1,2,0:T(8,128)(2,1)} %fusion.11) | data formatting | bytes 4194304
  297.5 8.8 %all-to-all-done = f32[16,2,2,16,256]{4,3,2,1,0:T(8,128)S(1)} async-done(((f32[16,2,2,16,256]{4,3,2,1,0:T(8,128)}), f32[16,2,2,16,256]{4,3,2,1,0:T(8,128)S(1)}, u32[]{:S(2)}, u32[]{:S(2)}) %all-to-all-start) | async-done | bytes 1048608 | tf_op jit(solution)/shard_map/all_to_all | solution.py:111
  (60 shorter events, 8.3 us)
Async XLA Ops:
  7.2 115.6 %copy-start = (bf16[1,4096,256]{2,1,0:T(8,128)(2,1)S(1)}, bf16[1,4096,256]{2,1,0:T(8,128)(2,1)}, u32[]{:S(2)}) copy-start(bf16[1,4096,256]{2,1,0:T(8,128)(2,1)} %param.12) | copy-start | bytes 6291460
  7.2 111.0 %all-gather.2.cloned.1.call-start = ((), (), s32[]{:S(2)}) async-start(), calls=%async_computation.2 | async-start | bytes 8912896 | tf_op jit(solution)/shard_map/all_gather | solution.py:63
  59.2 202.6 %reduce-scatter.2.cloned.1.call-start = ((), (), s32[]{:S(2)}) async-start(), calls=%async_computation.3 | async-start | bytes 8912896 | tf_op jit(solution)/shard_map/reduce_scatter | solution.py:104
  60.9 61.5 %copy-start.11 = (bf16[1,2,2,256,256]{4,3,2,1,0:T(8,128)(2,1)S(1)}, bf16[1,2,2,256,256]{4,3,2,1,0:T(8,128)(2,1)}, u32[]{:S(2)}) copy-start(bf16[1,2,2,256,256]{4,3,2,1,0:T(8,128)(2,1)} %param.11) | copy-start | bytes 1572868
  118.2 5.2 %copy-start.3 = (bf16[2,2,256,4096]{3,2,1,0:T(8,128)(2,1)S(1)}, bf16[2,2,256,4096]{3,2,1,0:T(8,128)(2,1)}, u32[]{:S(2)}) copy-start(bf16[2,2,256,4096]{3,2,1,0:T(8,128)(2,1)} %all-gather.2.cloned.1.call-done) | copy-start | bytes 25165828
  122.4 2.3 copy-start.13
  123.4 18.4 %copy-start.12 = (f32[2,256,256]{1,2,0:T(8,128)}, f32[2,256,256]{1,2,0:T(8,128)S(1)}, u32[]{:S(2)}) copy-start(f32[2,256,256]{1,2,0:T(8,128)S(1)} %fusion.84) | copy-start | bytes 1572868
  124.7 8.6 %copy-start.19 = (bf16[2,256,256]{2,1,0:T(8,128)(2,1)}, bf16[2,256,256]{2,1,0:T(8,128)(2,1)S(1)}, u32[]{:S(2)}) copy-start(bf16[2,256,256]{2,1,0:T(8,128)(2,1)S(1)} %fusion.51) | copy-start | bytes 786436
  133.3 4.6 %copy-start.15 = (bf16[2,256,256]{2,1,0:T(8,128)(2,1)}, bf16[2,256,256]{2,1,0:T(8,128)(2,1)S(1)}, u32[]{:S(2)}) copy-start(bf16[2,256,256]{2,1,0:T(8,128)(2,1)S(1)} %fusion.42) | copy-start | bytes 786436
  137.9 2.2 copy-start.21
  143.6 4.5 %copy-start.9 = (bf16[2,256,256]{2,1,0:T(8,128)(2,1)}, bf16[2,256,256]{2,1,0:T(8,128)(2,1)S(1)}, u32[]{:S(2)}) copy-start(bf16[2,256,256]{2,1,0:T(8,128)(2,1)S(1)} %convolution_convert_fusion.3) | copy-start | bytes 786436
  143.6 4.5 %copy-start.17 = (bf16[1,2,2,256,256]{4,3,2,1,0:T(8,128)(2,1)S(1)}, bf16[1,2,2,256,256]{4,3,2,1,0:T(8,128)(2,1)}, u32[]{:S(2)}) copy-start(bf16[1,2,2,256,256]{4,3,2,1,0:T(8,128)(2,1)} %param.10) | copy-start | bytes 1572868
  150.0 0.7 copy-start.7
  150.7 3.4 %copy-start.2 = (f32[2,256,4096]{2,1,0:T(8,128)S(1)}, f32[2,256,4096]{2,1,0:T(8,128)}, u32[]{:S(2)}) copy-start(f32[2,256,4096]{2,1,0:T(8,128)} %fusion.18) | copy-start | bytes 25165828
  150.7 4.0 %copy-start.4 = (bf16[1,4096,256]{2,1,0:T(8,128)(2,1)S(1)}, bf16[1,4096,256]{2,1,0:T(8,128)(2,1)}, u32[]{:S(2)}) copy-start(bf16[1,4096,256]{2,1,0:T(8,128)(2,1)} %param.13) | copy-start | bytes 6291460
  150.7 4.0 %copy-start.5 = (bf16[2,256,256]{1,2,0:T(8,128)(2,1)S(1)}, bf16[2,256,256]{1,2,0:T(8,128)(2,1)}, u32[]{:S(2)}) copy-start(bf16[2,256,256]{1,2,0:T(8,128)(2,1)} %fusion.60) | copy-start | bytes 786436
  165.6 0.9 copy-start.14
  165.6 1.1 copy-start.18
  165.6 1.2 copy-start.20
  165.6 1.8 copy-start.16
  165.6 1.8 copy-start.22
  171.2 104.0 %copy-start.8 = (bf16[2,256,256]{2,1,0:T(8,128)(2,1)S(1)}, bf16[2,256,256]{2,1,0:T(8,128)(2,1)}, u32[]{:S(2)}) copy-start(bf16[2,256,256]{2,1,0:T(8,128)(2,1)} %copy-done.7) | copy-start | bytes 786436
  264.0 42.3 %all-to-all-start = ((f32[16,2,2,16,256]{4,3,2,1,0:T(8,128)}), f32[16,2,2,16,256]{4,3,2,1,0:T(8,128)S(1)}, u32[]{:S(2)}, u32[]{:S(2)}) async-start(f32[16,2,2,16,256]{4,3,2,1,0:T(8,128)} %copy_bitcast_fusion), calls=%async_computation.1 | async-start | bytes 2097152 | tf_op jit(solution)/shard_map/all_to_all | solution.py:111
  275.2 3.6 %copy-start.10 = (bf16[2,256,256]{2,1,0:T(8,128)(2,1)S(1)}, bf16[2,256,256]{2,1,0:T(8,128)(2,1)}, u32[]{:S(2)}) copy-start(bf16[2,256,256]{2,1,0:T(8,128)(2,1)} %copy-done.9) | copy-start | bytes 786436
  284.9 3.5 %copy-start.6 = (bf16[2,256,256]{1,2,0:T(8,128)(2,1)S(1)}, bf16[2,256,256]{1,2,0:T(8,128)(2,1)}, u32[]{:S(2)}) copy-start(bf16[2,256,256]{1,2,0:T(8,128)(2,1)} %fusion.60) | copy-start | bytes 786436
  288.4 18.6 %copy-start.1 = (bf16[1,4096,256]{2,1,0:T(8,128)(2,1)S(1)}, bf16[1,4096,256]{2,1,0:T(8,128)(2,1)}, u32[]{:S(2)}) copy-start(bf16[1,4096,256]{2,1,0:T(8,128)(2,1)} %param.12) | copy-start | bytes 6291460
Sparse Core Ops, SparseCore 0:
  59.3 58.7 all-gather.1
  165.8 95.9 reduce-scatter.1

commit v4 on v3

--- a/solution.py
+++ b/solution.py
@@ -59,7 +59,12 @@
     key_acc = jnp.zeros(key_mat.shape, jnp.float32)
     value_acc = jnp.zeros(value_mat.shape, jnp.float32)
     attn_list, query_list, encoder_list = ([], [], [])
-    tall_enc = lax.all_gather(encoder_out, "dp", axis=2, tiled=True)
+    groups = lax.axis_size("dp")
+    copies = jnp.broadcast_to(encoder_out[None], (groups,) + encoder_out.shape)
+    from_each = lax.all_to_all(copies, "dp", 0, 0, tiled=True)
+    tall_enc = jnp.moveaxis(from_each, 0, 2).reshape(
+        encoder_out.shape[:2] + (groups * encoder_out.shape[2], encoder_out.shape[3])
+    )
     gathered_enc = lax.all_gather(tall_enc, "section", axis=3, tiled=True)
     for micro_idx in range(MICRO):
         whole_enc = gathered_enc[micro_idx]
@@ -104,7 +109,6 @@
     section_share = lax.psum_scatter(terms, "section", scatter_dimension=3, tiled=True)
     section_share = section_share.astype(jnp.float32)
     micro, enc_rows_all, examples_all, width_sec = section_share.shape
-    groups = lax.axis_size("dp")
     row_blocks = section_share.reshape(
         micro, groups, enc_rows_all // groups, examples_all, width_sec
     ).transpose(1, 0, 3, 2, 4)

time: 315 us -> 294 us (0.933)
  blocking collectives: 52 us -> 27.6 us
    all_gather x1 -> x0, blocking collectives: 52 us -> none  [body(): tall_enc = lax.all_gather(encoder_out, 'dp', axis=2, tiled=True)]
    all_to_all x0 -> x1, blocking collectives: none -> 27.6 us  [body(): from_each = lax.all_to_all(copies, 'dp', 0, 0, tiled=True)]
  transfers between devices with their start and end apart: 3 -> 3, of which waited for: 3 -> 3; matrix products, arithmetic and copies ran while one was open for 10% -> 11% of each run, Pallas kernels for 0% -> 0%
where the time goes in v4:
time: 294 us; the launch traced here: 293 us
  waiting for transfers between devices  157 us (53%)
  matrix products  57.9 us (20%)
  blocking collectives  27.6 us (9%)
  local copies, waits for them, and re-layouts  15.5 us (5%)
  between operations  14.4 us (5%)
  other arithmetic  11 us (4%)
  starting transfers between devices  10.3 us (4%)
    reduce_scatter x1, waiting for transfers between devices, body(): lax.psum_scatter(terms, 'section', scatter_dimension=3, tiled=True)  88.7 us
    all_gather x1, waiting for transfers between devices, body(): gathered_enc = lax.all_gather(tall_enc, 'section', axis=3, tiled=True)  59.1 us
    all_to_all x1, blocking collectives, body(): from_each = lax.all_to_all(copies, 'dp', 0, 0, tiled=True)  27.6 us
    unnamed x50, local copies, waits for them, and re-layouts  13.8 us
    all_to_all x1, starting transfers between devices, body(): received = lax.all_to_all(row_blocks, 'dp', 0, 0, tiled=True)  10.2 us
    all_to_all x1, waiting for transfers between devices, body(): received = lax.all_to_all(row_blocks, 'dp', 0, 0, tiled=True)  8.73 us
    dot_general x2, matrix products, body(): jnp.einsum('ekd,ekc->dc', whole_enc, value_flat, preferred_element_type=j...  8.57 us
    dot_general x2, matrix products, body(): jnp.einsum('ekd,dc->ekc', whole_enc, value_mat, preferred_element_type=jn...  8.36 us
  transfers between devices with their start and end apart: 3, of which 3 were waited for; matrix products, arithmetic and copies ran while one was open for 11% of the time, Pallas kernels for 0%

profile of v4, /device:TPU:32, one launch (start us, length us, event | category | flops | bytes accessed | tf_op | source)
XLA Modules:
  0.0 293.1 jit_solution(11936861422963676326)
XLA Ops:
  8.2 27.6 %all_to_all.10 = bf16[16,2,2,16,256]{4,3,2,1,0:T(8,128)(2,1)S(1)} all-to-all(bf16[16,2,2,16,256]{4,3,2,1,0:T(8,128)(2,1)S(1)} %broadcast_in_dim.88), channel_id=1, replica_groups=mesh['section'=16,'dp'=16] {'dp'}, dimensions={0} | all-to-all | bytes 1048576 | tf_op jit(solution)/shard_map/all_to_all | solution.py:64
  38.3 59.1 %all-gather.2.cloned.1.call-done = bf16[2,2,256,4096]{3,2,1,0:T(8,128)(2,1)} async-done(((bf16[2,2,256,256]{3,2,1,0:T(8,128)(2,1)}), bf16[2,2,256,4096]{3,2,1,0:T(8,128)(2,1)}) %all-gather.2.cloned.1.call-update) | async-done | bytes 8388624 | tf_op jit(solution)/shard_map/all_gather | solution.py:68
  97.4 4.2 %fusion.48 = bf16[2,256,256]{2,1,0:T(8,128)(2,1)S(1)} fusion(bf16[1,4096,256]{2,1,0:T(8,128)(2,1)} %param.13, bf16[2,2,256,4096]{3,2,1,0:T(8,128)(2,1)} %all-gather.2.cloned.1.call-done), kind=kOutput, calls=%fused_computation.57 | convolution fusion | flops 1073872896 | bytes 6553600 | tf_op jit(solution)/shard_map/ekd,dc->ekc/dot_general | solution.py:74
  102.6 1.3 fusion.51
  103.9 2.2 fusion.129
  106.1 2.3 fusion.60
  108.4 4.1 %fusion.42 = bf16[2,256,256]{2,1,0:T(8,128)(2,1)S(1)} fusion(bf16[1,4096,256]{2,1,0:T(8,128)(2,1)} %param.13, bf16[2,2,256,4096]{3,2,1,0:T(8,128)(2,1)} %all-gather.2.cloned.1.call-done), kind=kOutput, calls=%fused_computation.55 | convolution fusion | flops 1073872896 | bytes 6553600 | tf_op jit(solution)/shard_map/ekd,dc->ekc/dot_general | solution.py:74
  112.6 1.1 fusion.85
  113.7 3.4 %fusion.45 = bf16[2,256,256]{2,1,0:T(8,128)(2,1)S(1)} fusion(bf16[1,4096,256]{2,1,0:T(8,128)(2,1)S(1)} %copy-done, bf16[2,2,256,4096]{3,2,1,0:T(8,128)(2,1)} %all-gather.2.cloned.1.call-done), kind=kOutput, calls=%fused_computation.56 | convolution fusion | flops 1073872896 | bytes 6553600 | tf_op jit(solution)/shard_map/ekd,dc->ekc/dot_general | solution.py:71
  117.2 2.2 fusion.126
  119.4 1.7 fusion.61
  121.1 1.8 convolution_convert_fusion.3
  122.9 4.5 %fusion.18 = f32[2,256,4096]{2,1,0:T(8,128)} fusion(bf16[2,256,256]{2,1,0:T(8,128)(2,1)S(1)} %convolution_convert_fusion.3, bf16[1,4096,256]{2,1,0:T(8,128)(2,1)S(1)} %copy-done), kind=kOutput, calls=%fused_computation.27 | convolution fusion | flops 1073741824 | bytes 10747904 | tf_op jit(solution)/shard_map/ekc,dc->ked/dot_general | solution.py:97
  127.4 1.8 convolution_convert_fusion.2
  129.9 1.3 fusion.16
  131.2 2.1 copy-done.2
  133.9 1.3 fusion.4
  135.2 3.3 %fusion.5 = bf16[1,256,2,4096]{3,1,2,0:T(8,128)(2,1)} fusion(f32[2,256,4096]{2,1,0:T(8,128)S(1)} %fusion.16, bf16[2,256,256]{1,2,0:T(8,128)(2,1)S(1)} %fusion.61, bf16[1,4096,256]{2,1,0:T(8,128)(2,1)S(1)} %copy-done.4), kind=kOutput, calls=%fused_computation.8 | convolution fusion | flops 1077936128 | bytes 14942208 | tf_op jit(solution)/shard_map/ekc,dc->ked/dot_general | solution.py:99
  138.6 6.3 %pad_maximum_fusion = bf16[2,256,2,4096]{3,1,2,0:T(8,128)(2,1)} fusion(bf16[1,256,2,4096]{3,1,2,0:T(8,128)(2,1)} %fusion.5, bf16[1,256,2,4096]{3,1,2,0:T(8,128)(2,1)S(1)} %fusion.4), kind=kLoop, calls=%fused_computation.4 | loop fusion | flops 4194304 | bytes 16777216 | tf_op jit(solution)/shard_map/stack | solution.py:108
  147.4 1.0 copy.54
  148.4 2.1 fusion.58
  150.4 1.9 fusion.59
  152.4 88.7 %reduce-scatter.2.cloned.1.call-done = bf16[2,256,2,256]{3,1,2,0:T(8,128)(2,1)} async-done(((bf16[2,256,2,4096]{3,1,2,0:T(8,128)(2,1)}), bf16[2,256,2,256]{3,1,2,0:T(8,128)(2,1)}) %reduce-scatter.2.cloned.1.call-update) | async-done | bytes 524304 | tf_op jit(solution)/shard_map/reduce_scatter | solution.py:109
  241.1 2.2 copy_bitcast_fusion
  243.2 10.2 %all-to-all-start.1 = ((f32[16,2,2,16,256]{4,3,2,1,0:T(8,128)}), f32[16,2,2,16,256]{4,3,2,1,0:T(8,128)S(1)}, u32[]{:S(2)}, u32[]{:S(2)}) async-start(f32[16,2,2,16,256]{4,3,2,1,0:T(8,128)} %copy_bitcast_fusion), calls=%async_computation.2 | async-start | bytes 2097152 | tf_op jit(solution)/shard_map/all_to_all | solution.py:115
  254.5 3.6 %convolution_bitcast_fusion.2 = f32[256,4096]{1,0:T(8,128)S(1)} fusion(bf16[2,256,256]{2,1,0:T(8,128)(2,1)S(1)} %copy-done.8, bf16[2,2,256,4096]{3,2,1,0:T(8,128)(2,1)} %all-gather.2.cloned.1.call-done), kind=kOutput, calls=%fused_computation.11 | convolution fusion | flops 1073741824 | bytes 8650752 | tf_op jit(solution)/shard_map/ekd,ekc->dc/dot_general | solution.py:89
  258.0 3.6 %fusion.10 = bf16[1,4096,256]{1,2,0:T(8,128)(2,1)S(1)} fusion(f32[256,4096]{1,0:T(8,128)S(1)} %convolution_bitcast_fusion.2, bf16[2,256,256]{2,1,0:T(8,128)(2,1)S(1)} %copy-done.10, bf16[2,2,256,4096]{3,2,1,0:T(8,128)(2,1)} %all-gather.2.cloned.1.call-done), kind=kOutput, calls=%fused_computation.17 | convolution fusion | flops 1075838976 | bytes 10747904 | tf_op jit(solution)/shard_map/ekd,ekc->dc/dot_general | solution.py:89
  261.7 2.5 copy.56
  264.1 3.5 %convolution_bitcast_fusion = f32[256,4096]{1,0:T(8,128)S(1)} fusion(bf16[2,256,256]{1,2,0:T(8,128)(2,1)S(1)} %fusion.61, bf16[2,2,256,4096]{3,2,1,0:T(8,128)(2,1)} %all-gather.2.cloned.1.call-done), kind=kOutput, calls=%fused_computation.9 | convolution fusion | flops 1073741824 | bytes 8650752 | tf_op jit(solution)/shard_map/ekd,ekc->dc/dot_general | solution.py:92
  267.6 5.1 %fusion.11 = bf16[1,4096,256]{1,2,0:T(8,128)(2,1)} fusion(f32[256,4096]{1,0:T(8,128)S(1)} %convolution_bitcast_fusion, bf16[2,256,256]{1,2,0:T(8,128)(2,1)S(1)} %copy-done.6, bf16[2,2,256,4096]{3,2,1,0:T(8,128)(2,1)} %all-gather.2.cloned.1.call-done), kind=kOutput, calls=%fused_computation.18 | convolution fusion | flops 1075838976 | bytes 10747904 | tf_op jit(solution)/shard_map/ekd,ekc->dc/dot_general | solution.py:92
  272.7 4.1 %copy.57 = bf16[1,4096,256]{2,1,0:T(8,128)(2,1)} copy(bf16[1,4096,256]{1,2,0:T(8,128)(2,1)} %fusion.11) | data formatting | bytes 4194304
  276.8 8.7 %all-to-all-done.1 = f32[16,2,2,16,256]{4,3,2,1,0:T(8,128)S(1)} async-done(((f32[16,2,2,16,256]{4,3,2,1,0:T(8,128)}), f32[16,2,2,16,256]{4,3,2,1,0:T(8,128)S(1)}, u32[]{:S(2)}, u32[]{:S(2)}) %all-to-all-start.1) | async-done | bytes 1048608 | tf_op jit(solution)/shard_map/all_to_all | solution.py:115
  (62 shorter events, 10.0 us)
Async XLA Ops:
  7.2 94.9 %copy-start = (bf16[1,4096,256]{2,1,0:T(8,128)(2,1)S(1)}, bf16[1,4096,256]{2,1,0:T(8,128)(2,1)}, u32[]{:S(2)}) copy-start(bf16[1,4096,256]{2,1,0:T(8,128)(2,1)} %param.12) | copy-start | bytes 6291460
  7.2 90.2 %all-gather.2.cloned.1.call-start = ((), (), s32[]{:S(2)}) async-start(), calls=%async_computation.3 | async-start | bytes 8912896 | tf_op jit(solution)/shard_map/all_gather | solution.py:68
  36.6 204.5 %reduce-scatter.2.cloned.1.call-start = ((), (), s32[]{:S(2)}) async-start(), calls=%async_computation.4 | async-start | bytes 8912896 | tf_op jit(solution)/shard_map/reduce_scatter | solution.py:109
  38.3 63.3 %copy-start.11 = (bf16[1,2,2,256,256]{4,3,2,1,0:T(8,128)(2,1)S(1)}, bf16[1,2,2,256,256]{4,3,2,1,0:T(8,128)(2,1)}, u32[]{:S(2)}) copy-start(bf16[1,2,2,256,256]{4,3,2,1,0:T(8,128)(2,1)} %param.11) | copy-start | bytes 1572868
  97.4 5.2 %copy-start.3 = (bf16[2,2,256,4096]{3,2,1,0:T(8,128)(2,1)S(1)}, bf16[2,2,256,4096]{3,2,1,0:T(8,128)(2,1)}, u32[]{:S(2)}) copy-start(bf16[2,2,256,4096]{3,2,1,0:T(8,128)(2,1)} %all-gather.2.cloned.1.call-done) | copy-start | bytes 25165828
  101.6 2.3 copy-start.13
  102.6 18.4 %copy-start.12 = (f32[2,256,256]{1,2,0:T(8,128)}, f32[2,256,256]{1,2,0:T(8,128)S(1)}, u32[]{:S(2)}) copy-start(f32[2,256,256]{1,2,0:T(8,128)S(1)} %fusion.84) | copy-start | bytes 1572868
  103.9 8.6 %copy-start.19 = (bf16[2,256,256]{2,1,0:T(8,128)(2,1)}, bf16[2,256,256]{2,1,0:T(8,128)(2,1)S(1)}, u32[]{:S(2)}) copy-start(bf16[2,256,256]{2,1,0:T(8,128)(2,1)S(1)} %fusion.51) | copy-start | bytes 786436
  112.6 4.6 %copy-start.15 = (bf16[2,256,256]{2,1,0:T(8,128)(2,1)}, bf16[2,256,256]{2,1,0:T(8,128)(2,1)S(1)}, u32[]{:S(2)}) copy-start(bf16[2,256,256]{2,1,0:T(8,128)(2,1)S(1)} %fusion.42) | copy-start | bytes 786436
  117.2 2.2 copy-start.21
  122.8 4.5 %copy-start.9 = (bf16[2,256,256]{2,1,0:T(8,128)(2,1)}, bf16[2,256,256]{2,1,0:T(8,128)(2,1)S(1)}, u32[]{:S(2)}) copy-start(bf16[2,256,256]{2,1,0:T(8,128)(2,1)S(1)} %convolution_convert_fusion.3) | copy-start | bytes 786436
  122.8 4.5 %copy-start.17 = (bf16[1,2,2,256,256]{4,3,2,1,0:T(8,128)(2,1)S(1)}, bf16[1,2,2,256,256]{4,3,2,1,0:T(8,128)(2,1)}, u32[]{:S(2)}) copy-start(bf16[1,2,2,256,256]{4,3,2,1,0:T(8,128)(2,1)} %param.10) | copy-start | bytes 1572868
  129.2 0.7 copy-start.7
  129.9 3.4 %copy-start.2 = (f32[2,256,4096]{2,1,0:T(8,128)S(1)}, f32[2,256,4096]{2,1,0:T(8,128)}, u32[]{:S(2)}) copy-start(f32[2,256,4096]{2,1,0:T(8,128)} %fusion.18) | copy-start | bytes 25165828
  129.9 4.0 %copy-start.4 = (bf16[1,4096,256]{2,1,0:T(8,128)(2,1)S(1)}, bf16[1,4096,256]{2,1,0:T(8,128)(2,1)}, u32[]{:S(2)}) copy-start(bf16[1,4096,256]{2,1,0:T(8,128)(2,1)} %param.13) | copy-start | bytes 6291460
  129.9 4.0 %copy-start.5 = (bf16[2,256,256]{1,2,0:T(8,128)(2,1)S(1)}, bf16[2,256,256]{1,2,0:T(8,128)(2,1)}, u32[]{:S(2)}) copy-start(bf16[2,256,256]{1,2,0:T(8,128)(2,1)} %fusion.60) | copy-start | bytes 786436
  144.9 0.9 copy-start.14
  144.9 1.1 copy-start.18
  144.9 1.2 copy-start.20
  144.9 1.8 copy-start.16
  144.9 1.8 copy-start.22
  150.4 104.0 %copy-start.8 = (bf16[2,256,256]{2,1,0:T(8,128)(2,1)S(1)}, bf16[2,256,256]{2,1,0:T(8,128)(2,1)}, u32[]{:S(2)}) copy-start(bf16[2,256,256]{2,1,0:T(8,128)(2,1)} %copy-done.7) | copy-start | bytes 786436
  243.2 42.3 %all-to-all-start.1 = ((f32[16,2,2,16,256]{4,3,2,1,0:T(8,128)}), f32[16,2,2,16,256]{4,3,2,1,0:T(8,128)S(1)}, u32[]{:S(2)}, u32[]{:S(2)}) async-start(f32[16,2,2,16,256]{4,3,2,1,0:T(8,128)} %copy_bitcast_fusion), calls=%async_computation.2 | async-start | bytes 2097152 | tf_op jit(solution)/shard_map/all_to_all | solution.py:115
  254.5 3.6 %copy-start.10 = (bf16[2,256,256]{2,1,0:T(8,128)(2,1)S(1)}, bf16[2,256,256]{2,1,0:T(8,128)(2,1)}, u32[]{:S(2)}) copy-start(bf16[2,256,256]{2,1,0:T(8,128)(2,1)} %copy-done.9) | copy-start | bytes 786436
  264.1 3.5 %copy-start.6 = (bf16[2,256,256]{1,2,0:T(8,128)(2,1)S(1)}, bf16[2,256,256]{1,2,0:T(8,128)(2,1)}, u32[]{:S(2)}) copy-start(bf16[2,256,256]{1,2,0:T(8,128)(2,1)} %fusion.60) | copy-start | bytes 786436
  267.6 18.6 %copy-start.1 = (bf16[1,4096,256]{2,1,0:T(8,128)(2,1)S(1)}, bf16[1,4096,256]{2,1,0:T(8,128)(2,1)}, u32[]{:S(2)}) copy-start(bf16[1,4096,256]{2,1,0:T(8,128)(2,1)} %param.12) | copy-start | bytes 6291460
Sparse Core Ops, SparseCore 0:
  36.7 60.6 all-gather.1
  145.1 95.9 reduce-scatter.1

commit v5 on v4

--- a/solution.py
+++ b/solution.py
@@ -106,8 +106,12 @@
     key_grads = key_acc.astype(jnp.bfloat16)[None]
     value_grads = value_acc.astype(jnp.bfloat16)[None]
     terms = jnp.stack(encoder_list).astype(jnp.bfloat16)
-    section_share = lax.psum_scatter(terms, "section", scatter_dimension=3, tiled=True)
-    section_share = section_share.astype(jnp.float32)
+    sections = lax.axis_size("section")
+    feature_blocks = jnp.moveaxis(
+        terms.reshape(terms.shape[:3] + (sections, terms.shape[3] // sections)), 3, 0
+    )
+    from_sections = lax.all_to_all(feature_blocks, "section", 0, 0, tiled=True)
+    section_share = jnp.sum(from_sections.astype(jnp.float32), axis=0)
     micro, enc_rows_all, examples_all, width_sec = section_share.shape
     row_blocks = section_share.reshape(
         micro, groups, enc_rows_all // groups, examples_all, width_sec

time: 294 us -> 301 us (1.024)
  local copies, waits for them, and re-layouts: 15.5 us -> 23.7 us
  matrix products: 57.9 us -> 53.3 us
  starting transfers between devices: 10.3 us -> 13.5 us
    reduce_scatter x1 -> x0, waiting for transfers between devices: 88.7 us -> none  [body(): lax.psum_scatter(terms, 'section', scatter_dimension=3, tiled=True)]
    all_to_all x0 -> x1, waiting for transfers between devices: none -> 87.9 us  [body(): from_sections = lax.all_to_all(feature_blocks, 'section', 0, 0, tiled=True)]
    another operation x0 -> x2, local copies, waits for them, and re-layouts: none -> 7.28 us  [body(): terms = jnp.stack(encoder_list).astype(jnp.bfloat16)]
    another operation x1 -> x0, other arithmetic: 6.34 us -> none  [body(): terms = jnp.stack(encoder_list).astype(jnp.bfloat16)]
    all_to_all x0 -> x1, starting transfers between devices: none -> 5.27 us  [body(): from_sections = lax.all_to_all(feature_blocks, 'section', 0, 0, tiled=True)]
    reduce_sum x0 -> x1, other arithmetic: none -> 5.01 us  [body(): section_share = jnp.sum(from_sections.astype(jnp.float32), axis=0)]
    transpose x1, other arithmetic: 2.16 us -> 6.17 us  [body(): jnp.moveaxis(terms.reshape(terms.shape[:3] + (sections, terms.shape[3] //...]
    dot_general x2, matrix products: 5.79 us -> 2.57 us  [head_term(): jnp.einsum('ekc,dc->ked', key_flat, key_mat, preferred_element_type=jnp.f...]
  transfers between devices with their start and end apart: 3 -> 3, of which waited for: 3 -> 3; matrix products, arithmetic and copies ran while one was open for 11% -> 10% of each run, Pallas kernels for 0% -> 0%
where the time goes in v5:
time: 301 us; the launch traced here: 300 us
  waiting for transfers between devices  154 us (51%)
  matrix products  53.3 us (18%)
  blocking collectives  27.6 us (9%)
  local copies, waits for them, and re-layouts  23.7 us (8%)
  between operations  14.4 us (5%)
  starting transfers between devices  13.5 us (4%)
  other arithmetic  13.4 us (4%)
    all_to_all x1, waiting for transfers between devices, body(): from_sections = lax.all_to_all(feature_blocks, 'section', 0, 0, tiled=True)  87.9 us
    all_gather x1, waiting for transfers between devices, body(): gathered_enc = lax.all_gather(tall_enc, 'section', axis=3, tiled=True)  59.1 us
    all_to_all x1, blocking collectives, body(): from_each = lax.all_to_all(copies, 'dp', 0, 0, tiled=True)  27.6 us
    unnamed x53, local copies, waits for them, and re-layouts  12.8 us
    dot_general x2, matrix products, body(): jnp.einsum('ekd,ekc->dc', whole_enc, value_flat, preferred_element_type=j...  8.57 us
    dot_general x2, matrix products, body(): jnp.einsum('ekd,dc->ekc', whole_enc, value_mat, preferred_element_type=jn...  8.44 us
    all_to_all x1, starting transfers between devices, body(): received = lax.all_to_all(row_blocks, 'dp', 0, 0, tiled=True)  8.18 us
    all_to_all x1, waiting for transfers between devices, body(): received = lax.all_to_all(row_blocks, 'dp', 0, 0, tiled=True)  7.33 us
  transfers between devices with their start and end apart: 3, of which 3 were waited for; matrix products, arithmetic and copies ran while one was open for 10% of the time, Pallas kernels for 0%

profile of v5, /device:TPU:32, one launch (start us, length us, event | category | flops | bytes accessed | tf_op | source)
XLA Modules:
  0.0 300.2 jit_solution(12826540807571915377)
XLA Ops:
  8.2 27.6 %all_to_all.15 = bf16[16,2,2,16,256]{4,3,2,1,0:T(8,128)(2,1)S(1)} all-to-all(bf16[16,2,2,16,256]{4,3,2,1,0:T(8,128)(2,1)S(1)} %broadcast_in_dim.88), channel_id=1, replica_groups=mesh['section'=16,'dp'=16] {'dp'}, dimensions={0} | all-to-all | bytes 1048576 | tf_op jit(solution)/shard_map/all_to_all | solution.py:64
  38.3 59.1 %all-gather.2.cloned.1.call-done = bf16[2,2,256,4096]{3,2,1,0:T(8,128)(2,1)} async-done(((bf16[2,2,256,256]{3,2,1,0:T(8,128)(2,1)}), bf16[2,2,256,4096]{3,2,1,0:T(8,128)(2,1)}) %all-gather.2.cloned.1.call-update) | async-done | bytes 8388624 | tf_op jit(solution)/shard_map/all_gather | solution.py:68
  97.4 4.2 %fusion.46 = bf16[2,256,256]{2,1,0:T(8,128)(2,1)S(1)} fusion(bf16[1,4096,256]{2,1,0:T(8,128)(2,1)} %param.13, bf16[2,2,256,4096]{3,2,1,0:T(8,128)(2,1)} %all-gather.2.cloned.1.call-done), kind=kOutput, calls=%fused_computation.56 | convolution fusion | flops 1073872896 | bytes 6553600 | tf_op jit(solution)/shard_map/ekd,dc->ekc/dot_general | solution.py:74
  104.2 2.2 fusion.127
  106.4 1.6 fusion.58
  108.0 4.2 %fusion.40 = bf16[2,256,256]{2,1,0:T(8,128)(2,1)S(1)} fusion(bf16[1,4096,256]{2,1,0:T(8,128)(2,1)} %param.13, bf16[2,2,256,4096]{3,2,1,0:T(8,128)(2,1)} %all-gather.2.cloned.1.call-done), kind=kOutput, calls=%fused_computation.54 | convolution fusion | flops 1073872896 | bytes 6553600 | tf_op jit(solution)/shard_map/ekd,dc->ekc/dot_general | solution.py:74
  113.3 3.4 %fusion.43 = bf16[2,256,256]{2,1,0:T(8,128)(2,1)S(1)} fusion(bf16[1,4096,256]{2,1,0:T(8,128)(2,1)S(1)} %copy-done, bf16[2,2,256,4096]{3,2,1,0:T(8,128)(2,1)} %all-gather.2.cloned.1.call-done), kind=kOutput, calls=%fused_computation.55 | convolution fusion | flops 1073872896 | bytes 6553600 | tf_op jit(solution)/shard_map/ekd,dc->ekc/dot_general | solution.py:71
  116.8 2.2 fusion.124
  119.0 1.7 fusion.59
  120.7 2.0 convolution_convert_fusion.3
  124.4 1.4 add_convert_fusion.1
  125.7 1.4 copy.106
  127.2 3.8 %copy.80 = bf16[1,256,2,16,256]{4,1,2,0,3:T(8,128)(2,1)} copy(bf16[1,256,2,16,256]{4,3,1,2,0:T(8,128)(2,1)S(1)} %bitcast.250) | data formatting | bytes 8388608 | tf_op jit(solution)/shard_map/stack | solution.py:108
  130.9 1.9 convolution_convert_fusion.2
  134.6 1.4 add_convert_fusion
  135.9 1.4 copy.107
  137.4 3.5 %copy.81 = bf16[1,256,2,16,256]{4,1,2,0,3:T(8,128)(2,1)} copy(bf16[1,256,2,16,256]{4,3,1,2,0:T(8,128)(2,1)S(1)} %bitcast.251) | data formatting | bytes 8388608 | tf_op jit(solution)/shard_map/stack | solution.py:108
  140.9 6.2 %maximum_bitcast_fusion = bf16[16,2,256,2,256]{4,2,3,1,0:T(8,128)(2,1)} fusion(bf16[1,256,2,16,256]{4,1,2,0,3:T(8,128)(2,1)} %copy.81, bf16[1,256,2,16,256]{4,1,2,0,3:T(8,128)(2,1)S(1)} %copy-done.3), kind=kLoop, calls=%fused_computation.5 | loop fusion | flops 4194304 | bytes 16777216 | tf_op jit(solution)/shard_map/transpose | solution.py:110
  147.1 5.3 %all-to-all-start.1 = ((bf16[16,2,256,2,256]{4,2,3,1,0:T(8,128)(2,1)}), bf16[16,2,256,2,256]{4,2,3,1,0:T(8,128)(2,1)}, u32[]{:S(2)}, u32[]{:S(2)}) async-start(bf16[16,2,256,2,256]{4,2,3,1,0:T(8,128)(2,1)} %maximum_bitcast_fusion), calls=%async_computation.1 | async-start | bytes 16777216 | tf_op jit(solution)/shard_map/all_to_all | solution.py:113
  154.7 2.0 fusion.56
  156.7 2.0 fusion.57
  158.7 87.9 %all-to-all-done.1 = bf16[16,2,256,2,256]{4,2,3,1,0:T(8,128)(2,1)} async-done(((bf16[16,2,256,2,256]{4,2,3,1,0:T(8,128)(2,1)}), bf16[16,2,256,2,256]{4,2,3,1,0:T(8,128)(2,1)}, u32[]{:S(2)}, u32[]{:S(2)}) %all-to-all-start.1) | async-done | bytes 8388640 | tf_op jit(solution)/shard_map/all_to_all | solution.py:113
  246.5 5.0 %convert_reduce_fusion = f32[2,256,2,256]{3,1,2,0:T(8,128)S(1)} fusion(bf16[16,2,256,2,256]{4,2,3,1,0:T(8,128)(2,1)} %all-to-all-done.1), kind=kLoop, calls=%fused_computation.4 | loop fusion | flops 8126464 | bytes 9437184 | tf_op jit(solution)/shard_map/reduce_sum | solution.py:114
  251.6 1.8 copy.109
  253.4 8.2 %all-to-all-start.2 = ((f32[16,2,2,16,256]{4,2,3,1,0:T(2,128)}), f32[16,2,2,16,256]{4,2,3,1,0:T(2,128)S(1)}, u32[]{:S(2)}, u32[]{:S(2)}) async-start(f32[16,2,2,16,256]{4,2,3,1,0:T(2,128)} %bitcast.247), calls=%async_computation.2 | async-start | bytes 2097152 | tf_op jit(solution)/shard_map/all_to_all | solution.py:119
  262.6 3.6 %convolution_bitcast_fusion.2 = f32[256,4096]{1,0:T(8,128)S(1)} fusion(bf16[2,256,256]{2,1,0:T(8,128)(2,1)S(1)} %copy-done.9, bf16[2,2,256,4096]{3,2,1,0:T(8,128)(2,1)} %all-gather.2.cloned.1.call-done), kind=kOutput, calls=%fused_computation.10 | convolution fusion | flops 1073741824 | bytes 8650752 | tf_op jit(solution)/shard_map/ekd,ekc->dc/dot_general | solution.py:89
  266.2 3.6 %fusion.8 = bf16[1,4096,256]{1,2,0:T(8,128)(2,1)S(1)} fusion(f32[256,4096]{1,0:T(8,128)S(1)} %convolution_bitcast_fusion.2, bf16[2,256,256]{2,1,0:T(8,128)(2,1)S(1)} %copy-done.11, bf16[2,2,256,4096]{3,2,1,0:T(8,128)(2,1)} %all-gather.2.cloned.1.call-done), kind=kOutput, calls=%fused_computation.16 | convolution fusion | flops 1075838976 | bytes 10747904 | tf_op jit(solution)/shard_map/ekd,ekc->dc/dot_general | solution.py:89
  269.8 2.5 copy.86
  272.3 3.5 %convolution_bitcast_fusion = f32[256,4096]{1,0:T(8,128)S(1)} fusion(bf16[2,256,256]{1,2,0:T(8,128)(2,1)S(1)} %fusion.59, bf16[2,2,256,4096]{3,2,1,0:T(8,128)(2,1)} %all-gather.2.cloned.1.call-done), kind=kOutput, calls=%fused_computation.8 | convolution fusion | flops 1073741824 | bytes 8650752 | tf_op jit(solution)/shard_map/ekd,ekc->dc/dot_general | solution.py:92
  275.8 5.1 %fusion.9 = bf16[1,4096,256]{1,2,0:T(8,128)(2,1)} fusion(f32[256,4096]{1,0:T(8,128)S(1)} %convolution_bitcast_fusion, bf16[2,256,256]{1,2,0:T(8,128)(2,1)S(1)} %copy-done.7, bf16[2,2,256,4096]{3,2,1,0:T(8,128)(2,1)} %all-gather.2.cloned.1.call-done), kind=kOutput, calls=%fused_computation.17 | convolution fusion | flops 1075838976 | bytes 10747904 | tf_op jit(solution)/shard_map/ekd,ekc->dc/dot_general | solution.py:92
  280.9 4.1 %copy.87 = bf16[1,4096,256]{2,1,0:T(8,128)(2,1)} copy(bf16[1,4096,256]{1,2,0:T(8,128)(2,1)} %fusion.9) | data formatting | bytes 4194304
  284.9 7.3 %all-to-all-done.2 = f32[16,2,2,16,256]{4,2,3,1,0:T(2,128)S(1)} async-done(((f32[16,2,2,16,256]{4,2,3,1,0:T(2,128)}), f32[16,2,2,16,256]{4,2,3,1,0:T(2,128)S(1)}, u32[]{:S(2)}, u32[]{:S(2)}) %all-to-all-start.2) | async-done | bytes 1048608 | tf_op jit(solution)/shard_map/all_to_all | solution.py:119
  (67 shorter events, 14.9 us)
Async XLA Ops:
  7.2 95.7 %copy-start = (bf16[1,4096,256]{2,1,0:T(8,128)(2,1)S(1)}, bf16[1,4096,256]{2,1,0:T(8,128)(2,1)}, u32[]{:S(2)}) copy-start(bf16[1,4096,256]{2,1,0:T(8,128)(2,1)} %param.12) | copy-start | bytes 6291460
  7.2 90.2 %all-gather.2.cloned.1.call-start = ((), (), s32[]{:S(2)}) async-start(), calls=%async_computation.3 | async-start | bytes 8912896 | tf_op jit(solution)/shard_map/all_gather | solution.py:68
  38.3 63.4 %copy-start.12 = (bf16[1,2,2,256,256]{4,3,2,1,0:T(8,128)(2,1)S(1)}, bf16[1,2,2,256,256]{4,3,2,1,0:T(8,128)(2,1)}, u32[]{:S(2)}) copy-start(bf16[1,2,2,256,256]{4,3,2,1,0:T(8,128)(2,1)} %param.11) | copy-start | bytes 1572868
  97.4 5.5 %copy-start.2 = (bf16[2,2,256,4096]{3,2,1,0:T(8,128)(2,1)S(1)}, bf16[2,2,256,4096]{3,2,1,0:T(8,128)(2,1)}, u32[]{:S(2)}) copy-start(bf16[2,2,256,4096]{3,2,1,0:T(8,128)(2,1)} %all-gather.2.cloned.1.call-done) | copy-start | bytes 25165828
  101.6 2.5 copy-start.13
  104.2 8.0 %copy-start.19 = (bf16[2,256,256]{2,1,0:T(8,128)(2,1)}, bf16[2,256,256]{2,1,0:T(8,128)(2,1)S(1)}, u32[]{:S(2)}) copy-start(bf16[2,256,256]{2,1,0:T(8,128)(2,1)S(1)} %fusion.49) | copy-start | bytes 786436
  108.0 16.0 %copy-start.6 = (bf16[2,256,256]{1,2,0:T(8,128)(2,1)}, bf16[2,256,256]{1,2,0:T(8,128)(2,1)S(1)}, u32[]{:S(2)}) copy-start(bf16[2,256,256]{1,2,0:T(8,128)(2,1)S(1)} %fusion.58) | copy-start | bytes 786436
  112.2 4.6 %copy-start.15 = (bf16[2,256,256]{2,1,0:T(8,128)(2,1)}, bf16[2,256,256]{2,1,0:T(8,128)(2,1)S(1)}, u32[]{:S(2)}) copy-start(bf16[2,256,256]{2,1,0:T(8,128)(2,1)S(1)} %fusion.40) | copy-start | bytes 786436
  116.8 2.2 copy-start.21
  122.7 1.3 copy-start.10
  122.7 1.7 copy-start.4
  127.2 3.8 %copy-start.17 = (bf16[1,2,2,256,256]{4,3,2,1,0:T(8,128)(2,1)S(1)}, bf16[1,2,2,256,256]{4,3,2,1,0:T(8,128)(2,1)}, u32[]{:S(2)}) copy-start(bf16[1,2,2,256,256]{4,3,2,1,0:T(8,128)(2,1)} %param.10) | copy-start | bytes 1572868
  132.9 1.3 copy-start.8
  132.9 1.7 copy-start.5
  137.4 3.5 %copy-start.3 = (bf16[1,256,2,16,256]{4,1,2,0,3:T(8,128)(2,1)S(1)}, bf16[1,256,2,16,256]{4,1,2,0,3:T(8,128)(2,1)}, u32[]{:S(2)}) copy-start(bf16[1,256,2,16,256]{4,1,2,0,3:T(8,128)(2,1)} %copy.80) | copy-start | bytes 12582916
  147.1 5.3 %copy-start.14 = (bf16[2,256,256]{2,1,0:T(8,128)(2,1)S(1)}, bf16[2,256,256]{2,1,0:T(8,128)(2,1)}, u32[]{:S(2)}) copy-start(bf16[2,256,256]{2,1,0:T(8,128)(2,1)} %copy-done.13) | copy-start | bytes 786436
  147.1 5.3 %copy-start.18 = (bf16[1,2,2,256,256]{4,3,2,1,0:T(8,128)(2,1)S(1)}, bf16[1,2,2,256,256]{4,3,2,1,0:T(8,128)(2,1)}, u32[]{:S(2)}) copy-start(bf16[1,2,2,256,256]{4,3,2,1,0:T(8,128)(2,1)} %param.10) | copy-start | bytes 1572868
  147.1 5.3 %copy-start.20 = (bf16[2,256,256]{2,1,0:T(8,128)(2,1)S(1)}, bf16[2,256,256]{2,1,0:T(8,128)(2,1)}, u32[]{:S(2)}) copy-start(bf16[2,256,256]{2,1,0:T(8,128)(2,1)} %copy-done.19) | copy-start | bytes 786436
  147.1 5.9 %copy-start.16 = (bf16[2,256,256]{2,1,0:T(8,128)(2,1)S(1)}, bf16[2,256,256]{2,1,0:T(8,128)(2,1)}, u32[]{:S(2)}) copy-start(bf16[2,256,256]{2,1,0:T(8,128)(2,1)} %copy-done.15) | copy-start | bytes 786436
  147.1 5.9 %copy-start.22 = (bf16[2,256,256]{2,1,0:T(8,128)(2,1)S(1)}, bf16[2,256,256]{2,1,0:T(8,128)(2,1)}, u32[]{:S(2)}) copy-start(bf16[2,256,256]{2,1,0:T(8,128)(2,1)} %copy-done.21) | copy-start | bytes 786436
  147.1 99.4 %all-to-all-start.1 = ((bf16[16,2,256,2,256]{4,2,3,1,0:T(8,128)(2,1)}), bf16[16,2,256,2,256]{4,2,3,1,0:T(8,128)(2,1)}, u32[]{:S(2)}, u32[]{:S(2)}) async-start(bf16[16,2,256,2,256]{4,2,3,1,0:T(8,128)(2,1)} %maximum_bitcast_fusion), calls=%async_computation.1 | async-start | bytes 16777216 | tf_op jit(solution)/shard_map/all_to_all | solution.py:113
  251.5 11.1 %copy-start.9 = (bf16[2,256,256]{2,1,0:T(8,128)(2,1)S(1)}, bf16[2,256,256]{2,1,0:T(8,128)(2,1)}, u32[]{:S(2)}) copy-start(bf16[2,256,256]{2,1,0:T(8,128)(2,1)} %copy-done.8) | copy-start | bytes 786436
  253.4 38.9 %all-to-all-start.2 = ((f32[16,2,2,16,256]{4,2,3,1,0:T(2,128)}), f32[16,2,2,16,256]{4,2,3,1,0:T(2,128)S(1)}, u32[]{:S(2)}, u32[]{:S(2)}) async-start(f32[16,2,2,16,256]{4,2,3,1,0:T(2,128)} %bitcast.247), calls=%async_computation.2 | async-start | bytes 2097152 | tf_op jit(solution)/shard_map/all_to_all | solution.py:119
  262.6 3.6 %copy-start.11 = (bf16[2,256,256]{2,1,0:T(8,128)(2,1)S(1)}, bf16[2,256,256]{2,1,0:T(8,128)(2,1)}, u32[]{:S(2)}) copy-start(bf16[2,256,256]{2,1,0:T(8,128)(2,1)} %copy-done.10) | copy-start | bytes 786436
  272.3 3.5 %copy-start.7 = (bf16[2,256,256]{1,2,0:T(8,128)(2,1)S(1)}, bf16[2,256,256]{1,2,0:T(8,128)(2,1)}, u32[]{:S(2)}) copy-start(bf16[2,256,256]{1,2,0:T(8,128)(2,1)} %copy-done.6) | copy-start | bytes 786436
  275.8 17.5 %copy-start.1 = (bf16[1,4096,256]{2,1,0:T(8,128)(2,1)S(1)}, bf16[1,4096,256]{2,1,0:T(8,128)(2,1)}, u32[]{:S(2)}) copy-start(bf16[1,4096,256]{2,1,0:T(8,128)(2,1)} %param.12) | copy-start | bytes 6291460
Sparse Core Ops, SparseCore 0:
  36.7 60.6 all-gather.1

commit v6 on v5

--- a/solution.py
+++ b/solution.py
@@ -106,18 +106,19 @@
     key_grads = key_acc.astype(jnp.bfloat16)[None]
     value_grads = value_acc.astype(jnp.bfloat16)[None]
     terms = jnp.stack(encoder_list).astype(jnp.bfloat16)
+    micro, enc_rows_all, examples_all, width_all = terms.shape
+    groups = lax.axis_size("dp")
     sections = lax.axis_size("section")
+    row_blocks = jnp.moveaxis(
+        terms.reshape(micro, groups, enc_rows_all // groups, examples_all, width_all), 1, 0
+    )
+    from_heads = lax.all_to_all(row_blocks, "dp", 0, 0, tiled=True)
+    head_share = jnp.sum(from_heads.astype(jnp.float32), axis=0)
     feature_blocks = jnp.moveaxis(
-        terms.reshape(terms.shape[:3] + (sections, terms.shape[3] // sections)), 3, 0
+        head_share.reshape(head_share.shape[:3] + (sections, width_all // sections)), 3, 0
     )
     from_sections = lax.all_to_all(feature_blocks, "section", 0, 0, tiled=True)
-    section_share = jnp.sum(from_sections.astype(jnp.float32), axis=0)
-    micro, enc_rows_all, examples_all, width_sec = section_share.shape
-    row_blocks = section_share.reshape(
-        micro, groups, enc_rows_all // groups, examples_all, width_sec
-    ).transpose(1, 0, 3, 2, 4)
-    received = lax.all_to_all(row_blocks, "dp", 0, 0, tiled=True)
-    grad_encoder = jnp.sum(received, axis=0)
+    grad_encoder = jnp.transpose(jnp.sum(from_sections, axis=0), (0, 2, 1, 3))
     return (attention, query_grads, key_grads, value_grads, grad_encoder)
 
 

time: 301 us -> 393 us (1.31)
  the two profiles are of different devices: /device:TPU:32 before, /device:TPU:185 now
where the time goes in v6:
time: 393 us
  waiting for transfers between devices  239 us (61%)
  matrix products  57.7 us (15%)
  starting transfers between devices  33.2 us (8%)
  blocking collectives  20.3 us (5%)
  local copies, waits for them, and re-layouts  16.1 us (4%)
  between operations  14.4 us (4%)
  other arithmetic  12 us (3%)
    all_to_all x1, waiting for transfers between devices, body(): from_heads = lax.all_to_all(row_blocks, 'dp', 0, 0, tiled=True)  175 us
    all_gather x1, waiting for transfers between devices, body(): gathered_enc = lax.all_gather(tall_enc, 'section', axis=3, tiled=True)  64.1 us
    all_to_all x1, starting transfers between devices, body(): from_sections = lax.all_to_all(feature_blocks, 'section', 0, 0, tiled=True)  24 us
    all_to_all x1, blocking collectives, body(): from_each = lax.all_to_all(copies, 'dp', 0, 0, tiled=True)  20.3 us
    unnamed x46, local copies, waits for them, and re-layouts  12.5 us
    all_to_all x1, starting transfers between devices, body(): from_heads = lax.all_to_all(row_blocks, 'dp', 0, 0, tiled=True)  9.18 us
    dot_general x2, matrix products, body(): jnp.einsum('ekd,ekc->dc', whole_enc, value_flat, preferred_element_type=j...  8.57 us
    dot_general x2, matrix products, body(): jnp.einsum('ekd,dc->ekc', whole_enc, value_mat, preferred_element_type=jn...  8.44 us
  transfers between devices with their start and end apart: 3, of which 2 were waited for; matrix products, arithmetic and copies ran while one was open for 9% of the time, Pallas kernels for 0%

profile of v6, /device:TPU:185, one launch (start us, length us, event | category | flops | bytes accessed | tf_op | source)
XLA Modules:
  0.0 392.6 jit_solution(5475918916097969451)
XLA Ops:
  8.2 20.3 %all_to_all.15 = bf16[16,2,2,16,256]{4,3,2,1,0:T(8,128)(2,1)S(1)} all-to-all(bf16[16,2,2,16,256]{4,3,2,1,0:T(8,128)(2,1)S(1)} %broadcast_in_dim.88), channel_id=1, replica_groups=mesh['section'=16,'dp'=16] {'dp'}, dimensions={0} | all-to-all | bytes 1048576 | tf_op jit(solution)/shard_map/all_to_all | solution.py:64
  31.0 64.1 %all-gather.2.cloned.1.call-done = bf16[2,2,256,4096]{3,2,1,0:T(8,128)(2,1)} async-done(((bf16[2,2,256,256]{3,2,1,0:T(8,128)(2,1)}), bf16[2,2,256,4096]{3,2,1,0:T(8,128)(2,1)}) %all-gather.2.cloned.1.call-update) | async-done | bytes 8388624 | tf_op jit(solution)/shard_map/all_gather | solution.py:68
  95.1 4.2 %fusion.46 = bf16[2,256,256]{2,1,0:T(8,128)(2,1)S(1)} fusion(bf16[1,4096,256]{2,1,0:T(8,128)(2,1)} %param.13, bf16[2,2,256,4096]{3,2,1,0:T(8,128)(2,1)} %all-gather.2.cloned.1.call-done), kind=kOutput, calls=%fused_computation.57 | convolution fusion | flops 1073872896 | bytes 6553600 | tf_op jit(solution)/shard_map/ekd,dc->ekc/dot_general | solution.py:74
  99.3 1.2 fusion.82
  100.5 1.3 fusion.49
  101.8 2.2 fusion.127
  104.0 1.6 fusion.58
  105.6 4.2 %fusion.40 = bf16[2,256,256]{2,1,0:T(8,128)(2,1)S(1)} fusion(bf16[1,4096,256]{2,1,0:T(8,128)(2,1)} %param.13, bf16[2,2,256,4096]{3,2,1,0:T(8,128)(2,1)} %all-gather.2.cloned.1.call-done), kind=kOutput, calls=%fused_computation.55 | convolution fusion | flops 1073872896 | bytes 6553600 | tf_op jit(solution)/shard_map/ekd,dc->ekc/dot_general | solution.py:74
  111.0 3.4 fusion.43
  114.4 2.2 fusion.124
  116.6 1.7 fusion.59
  118.3 1.9 convolution_convert_fusion.3
  120.3 4.5 %fusion.16 = f32[2,256,4096]{2,1,0:T(8,128)} fusion(bf16[2,256,256]{2,1,0:T(8,128)(2,1)S(1)} %convolution_convert_fusion.3, bf16[1,4096,256]{2,1,0:T(8,128)(2,1)S(1)} %copy-done), kind=kOutput, calls=%fused_computation.27 | convolution fusion | flops 1073741824 | bytes 10747904 | tf_op jit(solution)/shard_map/ekc,dc->ked/dot_general | solution.py:97
  124.8 1.9 convolution_convert_fusion.2
  126.7 1.3 fusion.14
  128.0 2.1 copy-done.2
  130.7 1.4 add_convert_fusion.1
  132.3 1.4 add_convert_fusion
  133.7 3.8 copy_bitcast_fusion
  137.5 9.2 %all-to-all-start.1 = ((bf16[16,2,16,2,4096]{4,2,3,1,0:T(8,128)(2,1)}), bf16[16,2,16,2,4096]{4,2,3,1,0:T(8,128)(2,1)}, u32[]{:S(2)}, u32[]{:S(2)}) async-start(bf16[16,2,16,2,4096]{4,2,3,1,0:T(8,128)(2,1)} %copy_bitcast_fusion), calls=%async_computation.1 | async-start | bytes 16777216 | tf_op jit(solution)/shard_map/all_to_all | solution.py:115
  149.0 2.6 fusion.56
  151.6 2.7 fusion.57
  154.3 174.9 %all-to-all-done.1 = bf16[16,2,16,2,4096]{4,2,3,1,0:T(8,128)(2,1)} async-done(((bf16[16,2,16,2,4096]{4,2,3,1,0:T(8,128)(2,1)}), bf16[16,2,16,2,4096]{4,2,3,1,0:T(8,128)(2,1)}, u32[]{:S(2)}, u32[]{:S(2)}) %all-to-all-start.1) | async-done | bytes 8388640 | tf_op jit(solution)/shard_map/all_to_all | solution.py:115
  329.2 5.0 %convert_reduce_fusion = f32[2,16,2,4096]{3,1,2,0:T(8,128)S(1)} fusion(bf16[16,2,16,2,4096]{4,2,3,1,0:T(8,128)(2,1)} %all-to-all-done.1), kind=kLoop, calls=%fused_computation.4 | loop fusion | flops 8126464 | bytes 9437184 | tf_op jit(solution)/shard_map/reduce_sum | solution.py:116
  334.5 1.8 copy.110
  336.3 24.0 %all-to-all-start.2 = ((f32[16,2,16,2,256]{4,3,2,1,0:T(2,128)}), f32[16,2,16,2,256]{4,3,2,1,0:T(2,128)S(1)}, u32[]{:S(2)}, u32[]{:S(2)}) async-start(f32[16,2,16,2,256]{4,3,2,1,0:T(2,128)} %bitcast.246), calls=%async_computation.2 | async-start | bytes 2097152 | tf_op jit(solution)/shard_map/all_to_all | solution.py:120
  362.4 3.6 convolution_bitcast_fusion.2
  366.0 3.6 fusion.8
  369.6 2.5 copy.86
  372.1 3.5 convolution_bitcast_fusion
  375.6 5.1 %fusion.9 = bf16[1,4096,256]{1,2,0:T(8,128)(2,1)} fusion(f32[256,4096]{1,0:T(8,128)S(1)} %convolution_bitcast_fusion, bf16[2,256,256]{1,2,0:T(8,128)(2,1)S(1)} %copy-done.7, bf16[2,2,256,4096]{3,2,1,0:T(8,128)(2,1)} %all-gather.2.cloned.1.call-done), kind=kOutput, calls=%fused_computation.18 | convolution fusion | flops 1075838976 | bytes 10747904 | tf_op jit(solution)/shard_map/ekd,ekc->dc/dot_general | solution.py:92
  380.7 4.1 %copy.87 = bf16[1,4096,256]{2,1,0:T(8,128)(2,1)} copy(bf16[1,4096,256]{1,2,0:T(8,128)(2,1)} %fusion.9) | data formatting | bytes 4194304
  (58 shorter events, 11.2 us)
Async XLA Ops:
  7.2 93.4 %copy-start = (bf16[1,4096,256]{2,1,0:T(8,128)(2,1)S(1)}, bf16[1,4096,256]{2,1,0:T(8,128)(2,1)}, u32[]{:S(2)}) copy-start(bf16[1,4096,256]{2,1,0:T(8,128)(2,1)} %param.12) | copy-start | bytes 6291460
  7.2 87.9 %all-gather.2.cloned.1.call-start = ((), (), s32[]{:S(2)}) async-start(), calls=%async_computation.3 | async-start | bytes 8912896 | tf_op jit(solution)/shard_map/all_gather | solution.py:68
  31.0 68.3 %copy-start.12 = (bf16[1,2,2,256,256]{4,3,2,1,0:T(8,128)(2,1)S(1)}, bf16[1,2,2,256,256]{4,3,2,1,0:T(8,128)(2,1)}, u32[]{:S(2)}) copy-start(bf16[1,2,2,256,256]{4,3,2,1,0:T(8,128)(2,1)} %param.11) | copy-start | bytes 1572868
  95.1 5.5 %copy-start.3 = (bf16[2,2,256,4096]{3,2,1,0:T(8,128)(2,1)S(1)}, bf16[2,2,256,4096]{3,2,1,0:T(8,128)(2,1)}, u32[]{:S(2)}) copy-start(bf16[2,2,256,4096]{3,2,1,0:T(8,128)(2,1)} %all-gather.2.cloned.1.call-done) | copy-start | bytes 25165828
  101.8 8.0 %copy-start.16 = (bf16[2,256,256]{2,1,0:T(8,128)(2,1)}, bf16[2,256,256]{2,1,0:T(8,128)(2,1)S(1)}, u32[]{:S(2)}) copy-start(bf16[2,256,256]{2,1,0:T(8,128)(2,1)S(1)} %fusion.49) | copy-start | bytes 786436
  105.6 22.4 %copy-start.6 = (bf16[2,256,256]{1,2,0:T(8,128)(2,1)}, bf16[2,256,256]{1,2,0:T(8,128)(2,1)S(1)}, u32[]{:S(2)}) copy-start(bf16[2,256,256]{1,2,0:T(8,128)(2,1)S(1)} %fusion.58) | copy-start | bytes 786436
  109.8 4.6 %copy-start.13 = (bf16[2,256,256]{2,1,0:T(8,128)(2,1)}, bf16[2,256,256]{2,1,0:T(8,128)(2,1)S(1)}, u32[]{:S(2)}) copy-start(bf16[2,256,256]{2,1,0:T(8,128)(2,1)S(1)} %fusion.40) | copy-start | bytes 786436
  114.4 2.2 copy-start.18
  120.2 4.5 %copy-start.10 = (bf16[2,256,256]{2,1,0:T(8,128)(2,1)}, bf16[2,256,256]{2,1,0:T(8,128)(2,1)S(1)}, u32[]{:S(2)}) copy-start(bf16[2,256,256]{2,1,0:T(8,128)(2,1)S(1)} %convolution_convert_fusion.3) | copy-start | bytes 786436
  126.6 1.3 copy-start.8
  126.7 3.5 copy-start.2
  126.7 4.1 %copy-start.4 = (bf16[1,4096,256]{2,1,0:T(8,128)(2,1)S(1)}, bf16[1,4096,256]{2,1,0:T(8,128)(2,1)}, u32[]{:S(2)}) copy-start(bf16[1,4096,256]{2,1,0:T(8,128)(2,1)} %param.13) | copy-start | bytes 6291460
  130.7 1.6 copy-start.5
  137.5 9.2 %copy-start.15 = (bf16[1,2,2,256,256]{4,3,2,1,0:T(8,128)(2,1)S(1)}, bf16[1,2,2,256,256]{4,3,2,1,0:T(8,128)(2,1)}, u32[]{:S(2)}) copy-start(bf16[1,2,2,256,256]{4,3,2,1,0:T(8,128)(2,1)} %param.10) | copy-start | bytes 1572868
  137.5 9.2 %copy-start.17 = (bf16[2,256,256]{2,1,0:T(8,128)(2,1)S(1)}, bf16[2,256,256]{2,1,0:T(8,128)(2,1)}, u32[]{:S(2)}) copy-start(bf16[2,256,256]{2,1,0:T(8,128)(2,1)} %copy-done.16) | copy-start | bytes 786436
  137.5 9.8 %copy-start.14 = (bf16[2,256,256]{2,1,0:T(8,128)(2,1)S(1)}, bf16[2,256,256]{2,1,0:T(8,128)(2,1)}, u32[]{:S(2)}) copy-start(bf16[2,256,256]{2,1,0:T(8,128)(2,1)} %copy-done.13) | copy-start | bytes 786436
  137.5 9.8 %copy-start.19 = (bf16[2,256,256]{2,1,0:T(8,128)(2,1)S(1)}, bf16[2,256,256]{2,1,0:T(8,128)(2,1)}, u32[]{:S(2)}) copy-start(bf16[2,256,256]{2,1,0:T(8,128)(2,1)} %copy-done.18) | copy-start | bytes 786436
  137.5 191.7 %all-to-all-start.1 = ((bf16[16,2,16,2,4096]{4,2,3,1,0:T(8,128)(2,1)}), bf16[16,2,16,2,4096]{4,2,3,1,0:T(8,128)(2,1)}, u32[]{:S(2)}, u32[]{:S(2)}) async-start(bf16[16,2,16,2,4096]{4,2,3,1,0:T(8,128)(2,1)} %copy_bitcast_fusion), calls=%async_computation.1 | async-start | bytes 16777216 | tf_op jit(solution)/shard_map/all_to_all | solution.py:115
  334.5 27.9 %copy-start.9 = (bf16[2,256,256]{2,1,0:T(8,128)(2,1)S(1)}, bf16[2,256,256]{2,1,0:T(8,128)(2,1)}, u32[]{:S(2)}) copy-start(bf16[2,256,256]{2,1,0:T(8,128)(2,1)} %copy-done.8) | copy-start | bytes 786436
  336.3 48.4 %all-to-all-start.2 = ((f32[16,2,16,2,256]{4,3,2,1,0:T(2,128)}), f32[16,2,16,2,256]{4,3,2,1,0:T(2,128)S(1)}, u32[]{:S(2)}, u32[]{:S(2)}) async-start(f32[16,2,16,2,256]{4,3,2,1,0:T(2,128)} %bitcast.246), calls=%async_computation.2 | async-start | bytes 2097152 | tf_op jit(solution)/shard_map/all_to_all | solution.py:120
  362.4 3.6 copy-start.11
  372.1 3.5 copy-start.7
  375.6 10.2 %copy-start.1 = (bf16[1,4096,256]{2,1,0:T(8,128)(2,1)S(1)}, bf16[1,4096,256]{2,1,0:T(8,128)(2,1)}, u32[]{:S(2)}) copy-start(bf16[1,4096,256]{2,1,0:T(8,128)(2,1)} %param.12) | copy-start | bytes 6291460
Sparse Core Ops, SparseCore 0:
  29.4 65.5 all-gather.1

commit v7 on v4

--- a/solution.py
+++ b/solution.py
@@ -98,16 +98,20 @@
                 "ekc,dc->ked", key_flat, key_mat, preferred_element_type=jnp.float32
             ) + jnp.einsum("ekc,dc->ked", value_flat, value_mat, preferred_element_type=jnp.float32)
 
-        encoder_list.append(head_term(jnp.int32(0), lax.axis_size("dp") * rows_dev))
+        term = head_term(jnp.int32(0), lax.axis_size("dp") * rows_dev).astype(jnp.bfloat16)
+        sections = lax.axis_size("section")
+        feature_blocks = jnp.moveaxis(
+            term.reshape(term.shape[:2] + (sections, term.shape[2] // sections)), 2, 0
+        )
+        from_sections = lax.all_to_all(feature_blocks, "section", 0, 0, tiled=True)
+        encoder_list.append(jnp.sum(from_sections.astype(jnp.float32), axis=0))
         attn_list.append(attended.reshape(examples, dec_rows, width_dev))
         query_list.append(grad_query.reshape(examples, dec_rows, width_dev))
     attention = jnp.stack(attn_list)[None]
     query_grads = jnp.stack(query_list)[None]
     key_grads = key_acc.astype(jnp.bfloat16)[None]
     value_grads = value_acc.astype(jnp.bfloat16)[None]
-    terms = jnp.stack(encoder_list).astype(jnp.bfloat16)
-    section_share = lax.psum_scatter(terms, "section", scatter_dimension=3, tiled=True)
-    section_share = section_share.astype(jnp.float32)
+    section_share = jnp.stack(encoder_list)
     micro, enc_rows_all, examples_all, width_sec = section_share.shape
     row_blocks = section_share.reshape(
         micro, groups, enc_rows_all // groups, examples_all, width_sec

time: 294 us -> 276 us (0.939)
  waiting for transfers between devices: 157 us -> 134 us
  starting transfers between devices: 10.3 us -> 18.9 us
  matrix products: 57.9 us -> 53 us
    reduce_scatter x1 -> x0, waiting for transfers between devices: 88.7 us -> none  [body(): lax.psum_scatter(terms, 'section', scatter_dimension=3, tiled=True)]
    all_to_all x0 -> x2, waiting for transfers between devices: none -> 68.1 us  [body(): from_sections = lax.all_to_all(feature_blocks, 'section', 0, 0, tiled=True)]
    all_to_all x0 -> x2, starting transfers between devices: none -> 10.7 us  [body(): from_sections = lax.all_to_all(feature_blocks, 'section', 0, 0, tiled=True)]
    another operation x1 -> x0, other arithmetic: 6.34 us -> none  [body(): terms = jnp.stack(encoder_list).astype(jnp.bfloat16)]
    reduce_sum x0 -> x2, other arithmetic: none -> 5.65 us  [body(): encoder_list.append(jnp.sum(from_sections.astype(jnp.float32), axis=0))]
    reshape x0 -> x2, local copies, waits for them, and re-layouts: none -> 4.91 us  [body(): term.reshape(term.shape[:2] + (sections, term.shape[2] // sections))]
    unnamed x50 -> x45, local copies, waits for them, and re-layouts: 13.8 us -> 9.88 us
    dot_general x2, matrix products: 5.79 us -> 2.57 us  [head_term(): jnp.einsum('ekc,dc->ked', key_flat, key_mat, preferred_element_type=jnp.f...]
  transfers between devices with their start and end apart: 3 -> 4, of which waited for: 3 -> 4; matrix products, arithmetic and copies ran while one was open for 11% -> 20% of each run, Pallas kernels for 0% -> 0%
where the time goes in v7:
time: 276 us
  waiting for transfers between devices  134 us (49%)
  matrix products  53 us (19%)
  blocking collectives  27.6 us (10%)
  starting transfers between devices  18.9 us (7%)
  local copies, waits for them, and re-layouts  17.4 us (6%)
  between operations  14.4 us (5%)
  other arithmetic  10.6 us (4%)
    all_to_all x2, waiting for transfers between devices, body(): from_sections = lax.all_to_all(feature_blocks, 'section', 0, 0, tiled=True)  68.1 us
    all_gather x1, waiting for transfers between devices, body(): gathered_enc = lax.all_gather(tall_enc, 'section', axis=3, tiled=True)  59.1 us
    all_to_all x1, blocking collectives, body(): from_each = lax.all_to_all(copies, 'dp', 0, 0, tiled=True)  27.6 us
    all_to_all x2, starting transfers between devices, body(): from_sections = lax.all_to_all(feature_blocks, 'section', 0, 0, tiled=True)  10.7 us
    unnamed x45, local copies, waits for them, and re-layouts  9.88 us
    dot_general x2, matrix products, body(): jnp.einsum('ekd,ekc->dc', whole_enc, value_flat, preferred_element_type=j...  8.57 us
    dot_general x2, matrix products, body(): jnp.einsum('ekd,dc->ekc', whole_enc, value_mat, preferred_element_type=jn...  8.36 us
    all_to_all x1, starting transfers between devices, body(): received = lax.all_to_all(row_blocks, 'dp', 0, 0, tiled=True)  8.17 us
  transfers between devices with their start and end apart: 4, of which 4 were waited for; matrix products, arithmetic and copies ran while one was open for 20% of the time, Pallas kernels for 0%

profile of v7, /device:TPU:32, one launch (start us, length us, event | category | flops | bytes accessed | tf_op | source)
XLA Modules:
  0.0 275.5 jit_solution(4090158615953357684)
XLA Ops:
  8.2 27.6 %all_to_all.20 = bf16[16,2,2,16,256]{4,3,2,1,0:T(8,128)(2,1)S(1)} all-to-all(bf16[16,2,2,16,256]{4,3,2,1,0:T(8,128)(2,1)S(1)} %broadcast_in_dim.88), channel_id=1, replica_groups=mesh['section'=16,'dp'=16] {'dp'}, dimensions={0} | all-to-all | bytes 1048576 | tf_op jit(solution)/shard_map/all_to_all | solution.py:64
  38.3 59.1 %all-gather.2.cloned.1.call-done = bf16[2,2,256,4096]{3,2,1,0:T(8,128)(2,1)} async-done(((bf16[2,2,256,256]{3,2,1,0:T(8,128)(2,1)}), bf16[2,2,256,4096]{3,2,1,0:T(8,128)(2,1)}) %all-gather.2.cloned.1.call-update) | async-done | bytes 8388624 | tf_op jit(solution)/shard_map/all_gather | solution.py:68
  97.4 4.2 %fusion.46 = bf16[2,256,256]{2,1,0:T(8,128)(2,1)S(1)} fusion(bf16[1,4096,256]{2,1,0:T(8,128)(2,1)} %param.13, bf16[2,2,256,4096]{3,2,1,0:T(8,128)(2,1)} %all-gather.2.cloned.1.call-done), kind=kOutput, calls=%fused_computation.58 | convolution fusion | flops 1073872896 | bytes 6553600 | tf_op jit(solution)/shard_map/ekd,dc->ekc/dot_general | solution.py:74
  105.3 1.6 fusion.58
  106.9 2.1 convolution_convert_fusion.3
  110.6 1.4 add_convert_fusion.1
  112.0 2.4 copy.116
  114.5 4.9 %all-to-all-start.1 = ((bf16[16,256,2,256]{3,1,2,0:T(8,128)(2,1)}), bf16[16,256,2,256]{3,1,2,0:T(8,128)(2,1)}, u32[]{:S(2)}, u32[]{:S(2)}) async-start(bf16[16,256,2,256]{3,1,2,0:T(8,128)(2,1)} %bitcast.251), calls=%async_computation.1 | async-start | bytes 8388608 | tf_op jit(solution)/shard_map/all_to_all | solution.py:106
  119.4 4.1 %fusion.40 = bf16[2,256,256]{2,1,0:T(8,128)(2,1)S(1)} fusion(bf16[1,4096,256]{2,1,0:T(8,128)(2,1)} %param.13, bf16[2,2,256,4096]{3,2,1,0:T(8,128)(2,1)} %all-gather.2.cloned.1.call-done), kind=kOutput, calls=%fused_computation.56 | convolution fusion | flops 1073872896 | bytes 6553600 | tf_op jit(solution)/shard_map/ekd,dc->ekc/dot_general | solution.py:74
  124.7 3.4 %fusion.43 = bf16[2,256,256]{2,1,0:T(8,128)(2,1)S(1)} fusion(bf16[1,4096,256]{2,1,0:T(8,128)(2,1)S(1)} %copy-done, bf16[2,2,256,4096]{3,2,1,0:T(8,128)(2,1)} %all-gather.2.cloned.1.call-done), kind=kOutput, calls=%fused_computation.57 | convolution fusion | flops 1073872896 | bytes 6553600 | tf_op jit(solution)/shard_map/ekd,dc->ekc/dot_general | solution.py:71
  128.1 2.2 fusion.124
  130.3 2.0 convolution_convert_fusion.2
  132.3 1.8 fusion.59
  134.1 1.3 fusion.14
  135.7 1.4 add_convert_fusion
  137.0 2.5 copy.115
  139.5 29.1 %all-to-all-done.1 = bf16[16,256,2,256]{3,1,2,0:T(8,128)(2,1)} async-done(((bf16[16,256,2,256]{3,1,2,0:T(8,128)(2,1)}), bf16[16,256,2,256]{3,1,2,0:T(8,128)(2,1)}, u32[]{:S(2)}, u32[]{:S(2)}) %all-to-all-start.1) | async-done | bytes 4194336 | tf_op jit(solution)/shard_map/all_to_all | solution.py:106
  168.6 5.8 %all-to-all-start.2 = ((bf16[16,256,2,256]{3,1,2,0:T(8,128)(2,1)}), bf16[16,256,2,256]{3,1,2,0:T(8,128)(2,1)}, u32[]{:S(2)}, u32[]{:S(2)}) async-start(bf16[16,256,2,256]{3,1,2,0:T(8,128)(2,1)} %bitcast.250), calls=%async_computation.2 | async-start | bytes 8388608 | tf_op jit(solution)/shard_map/all_to_all | solution.py:106
  176.7 2.1 fusion.56
  178.8 2.6 fusion.57
  181.4 2.8 %convert_reduce_fusion.1 = f32[256,2,256]{2,0,1:T(8,128)S(1)} fusion(bf16[16,256,2,256]{3,1,2,0:T(8,128)(2,1)} %all-to-all-done.1), kind=kLoop, calls=%fused_computation.6 | loop fusion | flops 4063232 | bytes 4718592 | tf_op jit(solution)/shard_map/reduce_sum | solution.py:107
  184.7 39.0 %all-to-all-done.2 = bf16[16,256,2,256]{3,1,2,0:T(8,128)(2,1)} async-done(((bf16[16,256,2,256]{3,1,2,0:T(8,128)(2,1)}), bf16[16,256,2,256]{3,1,2,0:T(8,128)(2,1)}, u32[]{:S(2)}, u32[]{:S(2)}) %all-to-all-start.2) | async-done | bytes 4194336 | tf_op jit(solution)/shard_map/all_to_all | solution.py:106
  223.6 2.8 %convert_reduce_fusion = f32[256,2,256]{2,0,1:T(8,128)S(1)} fusion(bf16[16,256,2,256]{3,1,2,0:T(8,128)(2,1)} %all-to-all-done.2), kind=kLoop, calls=%fused_computation.4 | loop fusion | flops 4063232 | bytes 4718592 | tf_op jit(solution)/shard_map/reduce_sum | solution.py:107
  226.9 1.8 maximum_bitcast_fusion
  228.7 8.2 %all-to-all-start.3 = ((f32[16,2,2,16,256]{4,2,3,1,0:T(2,128)}), f32[16,2,2,16,256]{4,2,3,1,0:T(2,128)S(1)}, u32[]{:S(2)}, u32[]{:S(2)}) async-start(f32[16,2,2,16,256]{4,2,3,1,0:T(2,128)} %maximum_bitcast_fusion), calls=%async_computation.3 | async-start | bytes 2097152 | tf_op jit(solution)/shard_map/all_to_all | solution.py:119
  238.9 3.6 %convolution_bitcast_fusion.2 = f32[256,4096]{1,0:T(8,128)S(1)} fusion(bf16[2,256,256]{2,1,0:T(8,128)(2,1)S(1)} %copy-done.8, bf16[2,2,256,4096]{3,2,1,0:T(8,128)(2,1)} %all-gather.2.cloned.1.call-done), kind=kOutput, calls=%fused_computation.10 | convolution fusion | flops 1073741824 | bytes 8650752 | tf_op jit(solution)/shard_map/ekd,ekc->dc/dot_general | solution.py:89
  242.5 3.6 %fusion.8 = bf16[1,4096,256]{1,2,0:T(8,128)(2,1)S(1)} fusion(f32[256,4096]{1,0:T(8,128)S(1)} %convolution_bitcast_fusion.2, bf16[2,256,256]{2,1,0:T(8,128)(2,1)S(1)} %copy-done.10, bf16[2,2,256,4096]{3,2,1,0:T(8,128)(2,1)} %all-gather.2.cloned.1.call-done), kind=kOutput, calls=%fused_computation.16 | convolution fusion | flops 1075838976 | bytes 10747904 | tf_op jit(solution)/shard_map/ekd,ekc->dc/dot_general | solution.py:89
  246.1 2.5 copy.90
  248.6 3.5 %convolution_bitcast_fusion = f32[256,4096]{1,0:T(8,128)S(1)} fusion(bf16[2,256,256]{1,2,0:T(8,128)(2,1)S(1)} %fusion.59, bf16[2,2,256,4096]{3,2,1,0:T(8,128)(2,1)} %all-gather.2.cloned.1.call-done), kind=kOutput, calls=%fused_computation.8 | convolution fusion | flops 1073741824 | bytes 8650752 | tf_op jit(solution)/shard_map/ekd,ekc->dc/dot_general | solution.py:92
  252.1 5.1 %fusion.9 = bf16[1,4096,256]{1,2,0:T(8,128)(2,1)} fusion(f32[256,4096]{1,0:T(8,128)S(1)} %convolution_bitcast_fusion, bf16[2,256,256]{1,2,0:T(8,128)(2,1)S(1)} %copy-done.6, bf16[2,2,256,4096]{3,2,1,0:T(8,128)(2,1)} %all-gather.2.cloned.1.call-done), kind=kOutput, calls=%fused_computation.17 | convolution fusion | flops 1075838976 | bytes 10747904 | tf_op jit(solution)/shard_map/ekd,ekc->dc/dot_general | solution.py:92
  257.2 4.1 %copy.91 = bf16[1,4096,256]{2,1,0:T(8,128)(2,1)} copy(bf16[1,4096,256]{1,2,0:T(8,128)(2,1)} %fusion.9) | data formatting | bytes 4194304
  261.2 6.4 %all-to-all-done.3 = f32[16,2,2,16,256]{4,2,3,1,0:T(2,128)S(1)} async-done(((f32[16,2,2,16,256]{4,2,3,1,0:T(2,128)}), f32[16,2,2,16,256]{4,2,3,1,0:T(2,128)S(1)}, u32[]{:S(2)}, u32[]{:S(2)}) %all-to-all-start.3) | async-done | bytes 1048608 | tf_op jit(solution)/shard_map/all_to_all | solution.py:119
  (63 shorter events, 16.3 us)
Async XLA Ops:
  7.2 95.6 %copy-start = (bf16[1,4096,256]{2,1,0:T(8,128)(2,1)S(1)}, bf16[1,4096,256]{2,1,0:T(8,128)(2,1)}, u32[]{:S(2)}) copy-start(bf16[1,4096,256]{2,1,0:T(8,128)(2,1)} %param.12) | copy-start | bytes 6291460
  7.2 90.2 %all-gather.2.cloned.1.call-start = ((), (), s32[]{:S(2)}) async-start(), calls=%async_computation.4 | async-start | bytes 8912896 | tf_op jit(solution)/shard_map/all_gather | solution.py:68
  38.3 63.4 %copy-start.11 = (bf16[1,2,2,256,256]{4,3,2,1,0:T(8,128)(2,1)S(1)}, bf16[1,2,2,256,256]{4,3,2,1,0:T(8,128)(2,1)}, u32[]{:S(2)}) copy-start(bf16[1,2,2,256,256]{4,3,2,1,0:T(8,128)(2,1)} %param.11) | copy-start | bytes 1572868
  97.4 5.4 %copy-start.2 = (bf16[2,2,256,4096]{3,2,1,0:T(8,128)(2,1)S(1)}, bf16[2,2,256,4096]{3,2,1,0:T(8,128)(2,1)}, u32[]{:S(2)}) copy-start(bf16[2,2,256,4096]{3,2,1,0:T(8,128)(2,1)} %all-gather.2.cloned.1.call-done) | copy-start | bytes 25165828
  101.6 2.5 copy-start.12
  102.8 1.3 copy-start.14
  104.1 6.2 %copy-start.16 = (bf16[2,256,256]{2,1,0:T(8,128)(2,1)}, bf16[2,256,256]{2,1,0:T(8,128)(2,1)S(1)}, u32[]{:S(2)}) copy-start(bf16[2,256,256]{2,1,0:T(8,128)(2,1)S(1)} %fusion.49) | copy-start | bytes 786436
  106.9 3.4 %copy-start.5 = (bf16[2,256,256]{1,2,0:T(8,128)(2,1)}, bf16[2,256,256]{1,2,0:T(8,128)(2,1)S(1)}, u32[]{:S(2)}) copy-start(bf16[2,256,256]{1,2,0:T(8,128)(2,1)S(1)} %fusion.58) | copy-start | bytes 786436
  108.9 1.3 copy-start.9
  109.0 1.7 copy-start.3
  114.5 54.2 %all-to-all-start.1 = ((bf16[16,256,2,256]{3,1,2,0:T(8,128)(2,1)}), bf16[16,256,2,256]{3,1,2,0:T(8,128)(2,1)}, u32[]{:S(2)}, u32[]{:S(2)}) async-start(bf16[16,256,2,256]{3,1,2,0:T(8,128)(2,1)} %bitcast.251), calls=%async_computation.1 | async-start | bytes 8388608 | tf_op jit(solution)/shard_map/all_to_all | solution.py:106
  128.1 2.2 copy-start.18
  132.3 3.1 %copy-start.7 = (bf16[2,256,256]{2,1,0:T(8,128)(2,1)}, bf16[2,256,256]{2,1,0:T(8,128)(2,1)S(1)}, u32[]{:S(2)}) copy-start(bf16[2,256,256]{2,1,0:T(8,128)(2,1)S(1)} %convolution_convert_fusion.2) | copy-start | bytes 786436
  134.1 1.6 copy-start.4
  168.6 5.8 %copy-start.13 = (bf16[2,256,256]{2,1,0:T(8,128)(2,1)S(1)}, bf16[2,256,256]{2,1,0:T(8,128)(2,1)}, u32[]{:S(2)}) copy-start(bf16[2,256,256]{2,1,0:T(8,128)(2,1)} %copy-done.12) | copy-start | bytes 786436
  168.6 5.8 %copy-start.15 = (bf16[1,2,2,256,256]{4,3,2,1,0:T(8,128)(2,1)S(1)}, bf16[1,2,2,256,256]{4,3,2,1,0:T(8,128)(2,1)}, u32[]{:S(2)}) copy-start(bf16[1,2,2,256,256]{4,3,2,1,0:T(8,128)(2,1)} %param.10) | copy-start | bytes 1572868
  168.6 5.8 %copy-start.17 = (bf16[2,256,256]{2,1,0:T(8,128)(2,1)S(1)}, bf16[2,256,256]{2,1,0:T(8,128)(2,1)}, u32[]{:S(2)}) copy-start(bf16[2,256,256]{2,1,0:T(8,128)(2,1)} %copy-done.16) | copy-start | bytes 786436
  168.6 6.4 %copy-start.19 = (bf16[2,256,256]{2,1,0:T(8,128)(2,1)S(1)}, bf16[2,256,256]{2,1,0:T(8,128)(2,1)}, u32[]{:S(2)}) copy-start(bf16[2,256,256]{2,1,0:T(8,128)(2,1)} %copy-done.18) | copy-start | bytes 786436
  168.6 55.0 %all-to-all-start.2 = ((bf16[16,256,2,256]{3,1,2,0:T(8,128)(2,1)}), bf16[16,256,2,256]{3,1,2,0:T(8,128)(2,1)}, u32[]{:S(2)}, u32[]{:S(2)}) async-start(bf16[16,256,2,256]{3,1,2,0:T(8,128)(2,1)} %bitcast.250), calls=%async_computation.2 | async-start | bytes 8388608 | tf_op jit(solution)/shard_map/all_to_all | solution.py:106
  226.5 12.4 %copy-start.8 = (bf16[2,256,256]{2,1,0:T(8,128)(2,1)S(1)}, bf16[2,256,256]{2,1,0:T(8,128)(2,1)}, u32[]{:S(2)}) copy-start(bf16[2,256,256]{2,1,0:T(8,128)(2,1)} %copy-done.7) | copy-start | bytes 786436
  228.7 38.9 %all-to-all-start.3 = ((f32[16,2,2,16,256]{4,2,3,1,0:T(2,128)}), f32[16,2,2,16,256]{4,2,3,1,0:T(2,128)S(1)}, u32[]{:S(2)}, u32[]{:S(2)}) async-start(f32[16,2,2,16,256]{4,2,3,1,0:T(2,128)} %maximum_bitcast_fusion), calls=%async_computation.3 | async-start | bytes 2097152 | tf_op jit(solution)/shard_map/all_to_all | solution.py:119
  238.9 3.6 %copy-start.10 = (bf16[2,256,256]{2,1,0:T(8,128)(2,1)S(1)}, bf16[2,256,256]{2,1,0:T(8,128)(2,1)}, u32[]{:S(2)}) copy-start(bf16[2,256,256]{2,1,0:T(8,128)(2,1)} %copy-done.9) | copy-start | bytes 786436
  248.6 3.5 %copy-start.6 = (bf16[2,256,256]{1,2,0:T(8,128)(2,1)S(1)}, bf16[2,256,256]{1,2,0:T(8,128)(2,1)}, u32[]{:S(2)}) copy-start(bf16[2,256,256]{1,2,0:T(8,128)(2,1)} %copy-done.5) | copy-start | bytes 786436
  252.1 16.6 %copy-start.1 = (bf16[1,4096,256]{2,1,0:T(8,128)(2,1)S(1)}, bf16[1,4096,256]{2,1,0:T(8,128)(2,1)}, u32[]{:S(2)}) copy-start(bf16[1,4096,256]{2,1,0:T(8,128)(2,1)} %param.12) | copy-start | bytes 6291460
Sparse Core Ops, SparseCore 0:
  36.7 60.6 all-gather.1

commit v8 on v7

--- a/solution.py
+++ b/solution.py
@@ -65,7 +65,10 @@
     tall_enc = jnp.moveaxis(from_each, 0, 2).reshape(
         encoder_out.shape[:2] + (groups * encoder_out.shape[2], encoder_out.shape[3])
     )
-    gathered_enc = lax.all_gather(tall_enc, "section", axis=3, tiled=True)
+    gathered_enc = [
+        lax.all_gather(tall_enc[micro_idx], "section", axis=2, tiled=True)
+        for micro_idx in range(MICRO)
+    ]
     for micro_idx in range(MICRO):
         whole_enc = gathered_enc[micro_idx]
         key_rows = jnp.einsum(

time: 276 us -> 298 us (1.080)
  waiting for transfers between devices: 134 us -> 155 us
  matrix products: 53 us -> 48.1 us
  starting transfers between devices: 18.9 us -> 22 us
    all_gather x1 -> x2, waiting for transfers between devices: 59.1 us -> 108 us  [body(): lax.all_gather(tall_enc[micro_idx], 'section', axis=2, tiled=True)]
    all_to_all x2, waiting for transfers between devices: 68.1 us -> 38.5 us  [body(): from_sections = lax.all_to_all(feature_blocks, 'section', 0, 0, tiled=True)]
    all_to_all x2, starting transfers between devices: 10.7 us -> 14.5 us  [body(): from_sections = lax.all_to_all(feature_blocks, 'section', 0, 0, tiled=True)]
    unnamed x45 -> x51, local copies, waits for them, and re-layouts: 9.88 us -> 9.9 us
  transfers between devices with their start and end apart: 4 -> 5, of which waited for: 4 -> 4; matrix products, arithmetic and copies ran while one was open for 20% -> 23% of each run, Pallas kernels for 0% -> 0%
where the time goes in v8:
time: 298 us; the launch traced here: 297 us
  waiting for transfers between devices  155 us (52%)
  matrix products  48.1 us (16%)
  blocking collectives  27.6 us (9%)
  starting transfers between devices  22 us (7%)
  local copies, waits for them, and re-layouts  18 us (6%)
  between operations  14.4 us (5%)
  other arithmetic  11.7 us (4%)
    all_gather x2, waiting for transfers between devices, body(): lax.all_gather(tall_enc[micro_idx], 'section', axis=2, tiled=True)  108 us
    all_to_all x2, waiting for transfers between devices, body(): from_sections = lax.all_to_all(feature_blocks, 'section', 0, 0, tiled=True)  38.5 us
    all_to_all x1, blocking collectives, body(): from_each = lax.all_to_all(copies, 'dp', 0, 0, tiled=True)  27.6 us
    all_to_all x2, starting transfers between devices, body(): from_sections = lax.all_to_all(feature_blocks, 'section', 0, 0, tiled=True)  14.5 us
    unnamed x51, local copies, waits for them, and re-layouts  9.9 us
    all_to_all x1, waiting for transfers between devices, body(): received = lax.all_to_all(row_blocks, 'dp', 0, 0, tiled=True)  8.95 us
    dot_general x2, matrix products, body(): jnp.einsum('ekd,dc->ekc', whole_enc, value_mat, preferred_element_type=jn...  8.5 us
    all_to_all x1, starting transfers between devices, body(): received = lax.all_to_all(row_blocks, 'dp', 0, 0, tiled=True)  7.39 us
  transfers between devices with their start and end apart: 5, of which 4 were waited for; matrix products, arithmetic and copies ran while one was open for 23% of the time, Pallas kernels for 0%

profile of v8, /device:TPU:32, one launch (start us, length us, event | category | flops | bytes accessed | tf_op | source)
XLA Modules:
  0.0 297.1 jit_solution(2723752103407082301)
XLA Ops:
  8.2 27.6 %all_to_all.20 = bf16[16,2,2,16,256]{4,3,2,1,0:T(8,128)(2,1)S(1)} all-to-all(bf16[16,2,2,16,256]{4,3,2,1,0:T(8,128)(2,1)S(1)} %broadcast_in_dim.88), channel_id=1, replica_groups=mesh['section'=16,'dp'=16] {'dp'}, dimensions={0} | all-to-all | bytes 1048576 | tf_op jit(solution)/shard_map/all_to_all | solution.py:64
  39.0 42.1 %all-gather.3.cloned.1.call-done = bf16[2,256,4096]{2,1,0:T(8,128)(2,1)} async-done(((bf16[2,256,256]{2,1,0:T(8,128)(2,1)}), bf16[2,256,4096]{2,1,0:T(8,128)(2,1)}) %all-gather.3.cloned.1.call-update) | async-done | bytes 4194320 | tf_op jit(solution)/shard_map/all_gather | solution.py:69
  81.1 4.2 %fusion.40 = bf16[2,256,256]{2,1,0:T(8,128)(2,1)S(1)} fusion(bf16[2,256,4096]{2,1,0:T(8,128)(2,1)} %all-gather.3.cloned.1.call-done, bf16[1,4096,256]{2,1,0:T(8,128)(2,1)} %param.13), kind=kOutput, calls=%fused_computation.54 | convolution fusion | flops 1073872896 | bytes 6553600 | tf_op jit(solution)/shard_map/ekd,dc->ekc/dot_general | solution.py:77
  88.9 1.9 convolution_convert_fusion.3
  90.8 1.7 fusion.58
  94.2 1.4 add_convert_fusion.1
  95.6 2.4 copy.118
  98.1 6.4 %all-to-all-start.1 = ((bf16[16,256,2,256]{3,1,2,0:T(8,128)(2,1)}), bf16[16,256,2,256]{3,1,2,0:T(8,128)(2,1)}, u32[]{:S(2)}, u32[]{:S(2)}) async-start(bf16[16,256,2,256]{3,1,2,0:T(8,128)(2,1)} %bitcast.240), calls=%async_computation.1 | async-start | bytes 8388608 | tf_op jit(solution)/shard_map/all_to_all | solution.py:109
  104.4 65.7 %all-gather.5.cloned.1.call-done = bf16[2,256,4096]{2,1,0:T(8,128)(2,1)} async-done(((bf16[2,256,256]{2,1,0:T(8,128)(2,1)}), bf16[2,256,4096]{2,1,0:T(8,128)(2,1)}) %all-gather.5.cloned.1.call-update) | async-done | bytes 4194320 | tf_op jit(solution)/shard_map/all_gather | solution.py:69
  170.2 4.2 %fusion.43 = bf16[2,256,256]{2,1,0:T(8,128)(2,1)S(1)} fusion(bf16[2,256,4096]{2,1,0:T(8,128)(2,1)} %all-gather.5.cloned.1.call-done, bf16[1,4096,256]{2,1,0:T(8,128)(2,1)} %param.13), kind=kOutput, calls=%fused_computation.55 | convolution fusion | flops 1073872896 | bytes 6553600 | tf_op jit(solution)/shard_map/ekd,dc->ekc/dot_general | solution.py:77
  176.8 2.2 fusion.125
  179.0 2.2 convolution_convert_fusion.2
  181.3 1.8 fusion.59
  184.7 1.4 add_convert_fusion
  186.0 2.5 copy.117
  188.5 8.1 %all-to-all-start.2 = ((bf16[16,256,2,256]{3,1,2,0:T(8,128)(2,1)}), bf16[16,256,2,256]{3,1,2,0:T(8,128)(2,1)}, u32[]{:S(2)}, u32[]{:S(2)}) async-start(bf16[16,256,2,256]{3,1,2,0:T(8,128)(2,1)} %bitcast.239), calls=%async_computation.2 | async-start | bytes 8388608 | tf_op jit(solution)/shard_map/all_to_all | solution.py:109
  196.7 2.2 fusion.57
  198.9 2.6 fusion.56
  201.5 1.3 fusion.60
  202.8 1.3 fusion.61
  204.1 2.8 convert_reduce_fusion.1
  207.4 38.5 %all-to-all-done.2 = bf16[16,256,2,256]{3,1,2,0:T(8,128)(2,1)} async-done(((bf16[16,256,2,256]{3,1,2,0:T(8,128)(2,1)}), bf16[16,256,2,256]{3,1,2,0:T(8,128)(2,1)}, u32[]{:S(2)}, u32[]{:S(2)}) %all-to-all-start.2) | async-done | bytes 4194336 | tf_op jit(solution)/shard_map/all_to_all | solution.py:109
  245.9 2.8 convert_reduce_fusion
  249.1 1.9 maximum_bitcast_fusion
  251.1 7.4 %all-to-all-start.3 = ((f32[16,2,2,16,256]{4,2,3,1,0:T(2,128)}), f32[16,2,2,16,256]{4,2,3,1,0:T(2,128)S(1)}, u32[]{:S(2)}, u32[]{:S(2)}) async-start(f32[16,2,2,16,256]{4,2,3,1,0:T(2,128)} %maximum_bitcast_fusion), calls=%async_computation.3 | async-start | bytes 2097152 | tf_op jit(solution)/shard_map/all_to_all | solution.py:122
  262.6 3.6 %convolution_bitcast_fusion.2 = f32[256,4096]{1,0:T(8,128)S(1)} fusion(bf16[2,256,256]{2,1,0:T(8,128)(2,1)S(1)} %copy-done.11, bf16[2,256,4096]{2,1,0:T(8,128)(2,1)} %all-gather.5.cloned.1.call-done), kind=kOutput, calls=%fused_computation.10 | convolution fusion | flops 1073741824 | bytes 8650752 | tf_op jit(solution)/shard_map/ekd,ekc->dc/dot_general | solution.py:92
  266.2 1.3 fusion.8
  267.5 2.5 copy.92
  270.0 3.6 %convolution_bitcast_fusion = f32[256,4096]{1,0:T(8,128)S(1)} fusion(bf16[2,256,256]{1,2,0:T(8,128)(2,1)S(1)} %fusion.59, bf16[2,256,4096]{2,1,0:T(8,128)(2,1)} %all-gather.5.cloned.1.call-done), kind=kOutput, calls=%fused_computation.8 | convolution fusion | flops 1073741824 | bytes 8650752 | tf_op jit(solution)/shard_map/ekd,ekc->dc/dot_general | solution.py:95
  273.6 2.6 fusion.9
  276.2 4.1 %copy.93 = bf16[1,4096,256]{2,1,0:T(8,128)(2,1)} copy(bf16[1,4096,256]{1,2,0:T(8,128)(2,1)} %fusion.9) | data formatting | bytes 4194304
  280.3 9.0 %all-to-all-done.3 = f32[16,2,2,16,256]{4,2,3,1,0:T(2,128)S(1)} async-done(((f32[16,2,2,16,256]{4,2,3,1,0:T(2,128)}), f32[16,2,2,16,256]{4,2,3,1,0:T(2,128)S(1)}, u32[]{:S(2)}, u32[]{:S(2)}) %all-to-all-start.3) | async-done | bytes 1048608 | tf_op jit(solution)/shard_map/all_to_all | solution.py:122
  (74 shorter events, 19.4 us)
Async XLA Ops:
  7.2 79.3 %copy-start = (bf16[1,4096,256]{2,1,0:T(8,128)(2,1)S(1)}, bf16[1,4096,256]{2,1,0:T(8,128)(2,1)}, u32[]{:S(2)}) copy-start(bf16[1,4096,256]{2,1,0:T(8,128)(2,1)} %param.12) | copy-start | bytes 6291460
  7.2 73.9 %all-gather.3.cloned.1.call-start = ((), (), s32[]{:S(2)}) async-start(), calls=%async_computation.4 | async-start | bytes 4456448 | tf_op jit(solution)/shard_map/all_gather | solution.py:69
  36.5 133.6 %all-gather.5.cloned.1.call-start = ((), (), s32[]{:S(2)}) async-start(), calls=%async_computation.5 | async-start | bytes 4456448 | tf_op jit(solution)/shard_map/all_gather | solution.py:69
  39.0 46.4 %copy-start.14 = (bf16[1,2,2,256,256]{4,3,2,1,0:T(8,128)(2,1)S(1)}, bf16[1,2,2,256,256]{4,3,2,1,0:T(8,128)(2,1)}, u32[]{:S(2)}) copy-start(bf16[1,2,2,256,256]{4,3,2,1,0:T(8,128)(2,1)} %param.11) | copy-start | bytes 1572868
  81.1 5.4 %copy-start.3 = (bf16[2,256,4096]{2,1,0:T(8,128)(2,1)S(1)}, bf16[2,256,4096]{2,1,0:T(8,128)(2,1)}, u32[]{:S(2)}) copy-start(bf16[2,256,4096]{2,1,0:T(8,128)(2,1)} %all-gather.3.cloned.1.call-done) | copy-start | bytes 12582916
  85.3 2.4 copy-start.15
  86.5 1.3 copy-start.17
  87.8 6.1 %copy-start.19 = (bf16[2,256,256]{2,1,0:T(8,128)(2,1)}, bf16[2,256,256]{2,1,0:T(8,128)(2,1)S(1)}, u32[]{:S(2)}) copy-start(bf16[2,256,256]{2,1,0:T(8,128)(2,1)S(1)} %fusion.46) | copy-start | bytes 786436
  90.8 3.0 %copy-start.12 = (bf16[2,256,256]{2,1,0:T(8,128)(2,1)}, bf16[2,256,256]{2,1,0:T(8,128)(2,1)S(1)}, u32[]{:S(2)}) copy-start(bf16[2,256,256]{2,1,0:T(8,128)(2,1)S(1)} %convolution_convert_fusion.3) | copy-start | bytes 786436
  92.5 1.3 copy-start.8
  92.5 1.7 copy-start.6
  98.1 90.5 %all-to-all-start.1 = ((bf16[16,256,2,256]{3,1,2,0:T(8,128)(2,1)}), bf16[16,256,2,256]{3,1,2,0:T(8,128)(2,1)}, u32[]{:S(2)}, u32[]{:S(2)}) async-start(bf16[16,256,2,256]{3,1,2,0:T(8,128)(2,1)} %bitcast.240), calls=%async_computation.1 | async-start | bytes 8388608 | tf_op jit(solution)/shard_map/all_to_all | solution.py:109
  170.2 5.4 %copy-start.2 = (bf16[2,256,4096]{2,1,0:T(8,128)(2,1)S(1)}, bf16[2,256,4096]{2,1,0:T(8,128)(2,1)}, u32[]{:S(2)}) copy-start(bf16[2,256,4096]{2,1,0:T(8,128)(2,1)} %all-gather.5.cloned.1.call-done) | copy-start | bytes 12582916
  176.8 2.2 copy-start.21
  181.3 3.1 %copy-start.10 = (bf16[2,256,256]{2,1,0:T(8,128)(2,1)}, bf16[2,256,256]{2,1,0:T(8,128)(2,1)S(1)}, u32[]{:S(2)}) copy-start(bf16[2,256,256]{2,1,0:T(8,128)(2,1)S(1)} %convolution_convert_fusion.2) | copy-start | bytes 786436
  183.1 1.6 copy-start.7
  188.5 8.2 %copy-start.22 = (bf16[2,256,256]{2,1,0:T(8,128)(2,1)S(1)}, bf16[2,256,256]{2,1,0:T(8,128)(2,1)}, u32[]{:S(2)}) copy-start(bf16[2,256,256]{2,1,0:T(8,128)(2,1)} %copy-done.21) | copy-start | bytes 786436
  188.5 10.4 %copy-start.20 = (bf16[2,256,256]{2,1,0:T(8,128)(2,1)S(1)}, bf16[2,256,256]{2,1,0:T(8,128)(2,1)}, u32[]{:S(2)}) copy-start(bf16[2,256,256]{2,1,0:T(8,128)(2,1)} %copy-done.19) | copy-start | bytes 786436
  188.5 57.4 %all-to-all-start.2 = ((bf16[16,256,2,256]{3,1,2,0:T(8,128)(2,1)}), bf16[16,256,2,256]{3,1,2,0:T(8,128)(2,1)}, u32[]{:S(2)}, u32[]{:S(2)}) async-start(bf16[16,256,2,256]{3,1,2,0:T(8,128)(2,1)} %bitcast.239), calls=%async_computation.2 | async-start | bytes 8388608 | tf_op jit(solution)/shard_map/all_to_all | solution.py:109
  196.7 4.9 %copy-start.18 = (bf16[1,2,2,256,256]{4,3,2,1,0:T(8,128)(2,1)S(1)}, bf16[1,2,2,256,256]{4,3,2,1,0:T(8,128)(2,1)}, u32[]{:S(2)}) copy-start(bf16[1,2,2,256,256]{4,3,2,1,0:T(8,128)(2,1)} %param.10) | copy-start | bytes 1572868
  196.7 6.2 %copy-start.16 = (bf16[2,256,256]{2,1,0:T(8,128)(2,1)S(1)}, bf16[2,256,256]{2,1,0:T(8,128)(2,1)}, u32[]{:S(2)}) copy-start(bf16[2,256,256]{2,1,0:T(8,128)(2,1)} %copy-done.15) | copy-start | bytes 786436
  249.1 13.4 %copy-start.11 = (bf16[2,256,256]{2,1,0:T(8,128)(2,1)S(1)}, bf16[2,256,256]{2,1,0:T(8,128)(2,1)}, u32[]{:S(2)}) copy-start(bf16[2,256,256]{2,1,0:T(8,128)(2,1)} %copy-done.10) | copy-start | bytes 786436
  251.1 38.2 %all-to-all-start.3 = ((f32[16,2,2,16,256]{4,2,3,1,0:T(2,128)}), f32[16,2,2,16,256]{4,2,3,1,0:T(2,128)S(1)}, u32[]{:S(2)}, u32[]{:S(2)}) async-start(f32[16,2,2,16,256]{4,2,3,1,0:T(2,128)} %maximum_bitcast_fusion), calls=%async_computation.3 | async-start | bytes 2097152 | tf_op jit(solution)/shard_map/all_to_all | solution.py:122
  262.6 3.6 %copy-start.4 = (bf16[2,256,4096]{2,1,0:T(8,128)(2,1)S(1)}, bf16[2,256,4096]{2,1,0:T(8,128)(2,1)}, u32[]{:S(2)}) copy-start(bf16[2,256,4096]{2,1,0:T(8,128)(2,1)} %all-gather.3.cloned.1.call-done) | copy-start | bytes 12582916
  262.6 3.6 %copy-start.13 = (bf16[2,256,256]{2,1,0:T(8,128)(2,1)S(1)}, bf16[2,256,256]{2,1,0:T(8,128)(2,1)}, u32[]{:S(2)}) copy-start(bf16[2,256,256]{2,1,0:T(8,128)(2,1)} %copy-done.12) | copy-start | bytes 786436
  269.9 3.6 %copy-start.5 = (bf16[2,256,4096]{2,1,0:T(8,128)(2,1)S(1)}, bf16[2,256,4096]{2,1,0:T(8,128)(2,1)}, u32[]{:S(2)}) copy-start(bf16[2,256,4096]{2,1,0:T(8,128)(2,1)} %all-gather.3.cloned.1.call-done) | copy-start | bytes 12582916
  270.0 3.6 %copy-start.9 = (bf16[2,256,256]{1,2,0:T(8,128)(2,1)S(1)}, bf16[2,256,256]{1,2,0:T(8,128)(2,1)}, u32[]{:S(2)}) copy-start(bf16[2,256,256]{1,2,0:T(8,128)(2,1)} %copy-done.8) | copy-start | bytes 786436
  273.6 16.7 %copy-start.1 = (bf16[1,4096,256]{2,1,0:T(8,128)(2,1)S(1)}, bf16[1,4096,256]{2,1,0:T(8,128)(2,1)}, u32[]{:S(2)}) copy-start(bf16[1,4096,256]{2,1,0:T(8,128)(2,1)} %param.12) | copy-start | bytes 6291460
Sparse Core Ops, SparseCore 0:
  36.6 44.3 all-gather.2
  83.4 86.7 all-gather.4

commit v9 on v7

--- a/solution.py
+++ b/solution.py
@@ -93,16 +93,15 @@
             "ekd,ekc->dc", whole_enc, value_flat, preferred_element_type=jnp.float32
         )
 
-        def head_term(first_row, row_count, key_flat=key_flat, value_flat=value_flat):
-            return jnp.einsum(
-                "ekc,dc->ked", key_flat, key_mat, preferred_element_type=jnp.float32
-            ) + jnp.einsum("ekc,dc->ked", value_flat, value_mat, preferred_element_type=jnp.float32)
-
-        term = head_term(jnp.int32(0), lax.axis_size("dp") * rows_dev).astype(jnp.bfloat16)
         sections = lax.axis_size("section")
-        feature_blocks = jnp.moveaxis(
-            term.reshape(term.shape[:2] + (sections, term.shape[2] // sections)), 2, 0
-        )
+        key_blocks = key_mat.reshape(sections, key_mat.shape[0] // sections, width_dev)
+        value_blocks = value_mat.reshape(sections, value_mat.shape[0] // sections, width_dev)
+        feature_blocks = (
+            jnp.einsum("ekc,fdc->fked", key_flat, key_blocks, preferred_element_type=jnp.float32)
+            + jnp.einsum(
+                "ekc,fdc->fked", value_flat, value_blocks, preferred_element_type=jnp.float32
+            )
+        ).astype(jnp.bfloat16)
         from_sections = lax.all_to_all(feature_blocks, "section", 0, 0, tiled=True)
         encoder_list.append(jnp.sum(from_sections.astype(jnp.float32), axis=0))
         attn_list.append(attended.reshape(examples, dec_rows, width_dev))

time: 276 us -> 276 us (level)
    reshape x2 -> x0, local copies, waits for them, and re-layouts: 4.91 us -> none  [body(): term.reshape(term.shape[:2] + (sections, term.shape[2] // sections))]
    convert_element_type x0 -> x2, local copies, waits for them, and re-layouts: none -> 4.44 us  [body(): feature_blocks = (jnp.einsum('ekc,fdc->fked', key_flat, key_blocks, prefe...]
where the time goes in v9:
time: 276 us; the launch traced here: 275 us
  waiting for transfers between devices  134 us (49%)
  matrix products  52.9 us (19%)
  blocking collectives  27.6 us (10%)
  starting transfers between devices  18.8 us (7%)
  local copies, waits for them, and re-layouts  16.9 us (6%)
  between operations  14.4 us (5%)
  other arithmetic  10.6 us (4%)
    all_to_all x2, waiting for transfers between devices, body(): from_sections = lax.all_to_all(feature_blocks, 'section', 0, 0, tiled=True)  68.4 us
    all_gather x1, waiting for transfers between devices, body(): gathered_enc = lax.all_gather(tall_enc, 'section', axis=3, tiled=True)  59.1 us
    all_to_all x1, blocking collectives, body(): from_each = lax.all_to_all(copies, 'dp', 0, 0, tiled=True)  27.6 us
    all_to_all x2, starting transfers between devices, body(): from_sections = lax.all_to_all(feature_blocks, 'section', 0, 0, tiled=True)  10.6 us
    unnamed x45, local copies, waits for them, and re-layouts  9.88 us
    dot_general x2, matrix products, body(): jnp.einsum('ekd,ekc->dc', whole_enc, value_flat, preferred_element_type=j...  8.57 us
    dot_general x2, matrix products, body(): jnp.einsum('ekd,dc->ekc', whole_enc, value_mat, preferred_element_type=jn...  8.36 us
    all_to_all x1, starting transfers between devices, body(): received = lax.all_to_all(row_blocks, 'dp', 0, 0, tiled=True)  8.18 us
  transfers between devices with their start and end apart: 4, of which 4 were waited for; matrix products, arithmetic and copies ran while one was open for 20% of the time, Pallas kernels for 0%

profile of v9, /device:TPU:32, one launch (start us, length us, event | category | flops | bytes accessed | tf_op | source)
XLA Modules:
  0.0 275.1 jit_solution(1751855742102394611)
XLA Ops:
  8.2 27.6 %all_to_all.20 = bf16[16,2,2,16,256]{4,3,2,1,0:T(8,128)(2,1)S(1)} all-to-all(bf16[16,2,2,16,256]{4,3,2,1,0:T(8,128)(2,1)S(1)} %broadcast_in_dim.88), channel_id=1, replica_groups=mesh['section'=16,'dp'=16] {'dp'}, dimensions={0} | all-to-all | bytes 1048576 | tf_op jit(solution)/shard_map/all_to_all | solution.py:64
  38.3 59.1 %all-gather.2.cloned.1.call-done = bf16[2,2,256,4096]{3,2,1,0:T(8,128)(2,1)} async-done(((bf16[2,2,256,256]{3,2,1,0:T(8,128)(2,1)}), bf16[2,2,256,4096]{3,2,1,0:T(8,128)(2,1)}) %all-gather.2.cloned.1.call-update) | async-done | bytes 8388624 | tf_op jit(solution)/shard_map/all_gather | solution.py:68
  97.4 4.2 %fusion.42 = bf16[2,256,256]{2,1,0:T(8,128)(2,1)S(1)} fusion(bf16[1,4096,256]{2,1,0:T(8,128)(2,1)} %param.13, bf16[2,2,256,4096]{3,2,1,0:T(8,128)(2,1)} %all-gather.2.cloned.1.call-done), kind=kOutput, calls=%fused_computation.52 | convolution fusion | flops 1073872896 | bytes 6553600 | tf_op jit(solution)/shard_map/ekd,dc->ekc/dot_general | solution.py:74
  105.3 1.6 convolution_convert_fusion.1
  106.9 2.1 convolution_convert_fusion.3
  110.6 1.3 fusion.10
  112.0 2.2 copy.81
  114.2 4.9 %all-to-all-start.1 = ((bf16[16,256,2,256]{3,1,2,0:T(8,128)(2,1)}), bf16[16,256,2,256]{3,1,2,0:T(8,128)(2,1)}, u32[]{:S(2)}, u32[]{:S(2)}) async-start(bf16[16,256,2,256]{3,1,2,0:T(8,128)(2,1)} %copy.81), calls=%async_computation.1 | async-start | bytes 8388608 | tf_op jit(solution)/shard_map/all_to_all | solution.py:105
  119.1 4.1 %fusion.36 = bf16[2,256,256]{2,1,0:T(8,128)(2,1)S(1)} fusion(bf16[1,4096,256]{2,1,0:T(8,128)(2,1)} %param.13, bf16[2,2,256,4096]{3,2,1,0:T(8,128)(2,1)} %all-gather.2.cloned.1.call-done), kind=kOutput, calls=%fused_computation.50 | convolution fusion | flops 1073872896 | bytes 6553600 | tf_op jit(solution)/shard_map/ekd,dc->ekc/dot_general | solution.py:74
  124.4 3.4 %fusion.39 = bf16[2,256,256]{2,1,0:T(8,128)(2,1)S(1)} fusion(bf16[1,4096,256]{2,1,0:T(8,128)(2,1)S(1)} %copy-done, bf16[2,2,256,4096]{3,2,1,0:T(8,128)(2,1)} %all-gather.2.cloned.1.call-done), kind=kOutput, calls=%fused_computation.51 | convolution fusion | flops 1073872896 | bytes 6553600 | tf_op jit(solution)/shard_map/ekd,dc->ekc/dot_general | solution.py:71
  127.8 2.2 fusion.126
  130.0 2.0 convolution_convert_fusion.2
  132.0 1.8 convolution_convert_fusion
  133.8 1.3 fusion.66
  135.4 1.3 fusion.11
  136.7 2.2 copy.84
  139.0 29.4 %all-to-all-done.1 = bf16[16,256,2,256]{3,1,2,0:T(8,128)(2,1)} async-done(((bf16[16,256,2,256]{3,1,2,0:T(8,128)(2,1)}), bf16[16,256,2,256]{3,1,2,0:T(8,128)(2,1)}, u32[]{:S(2)}, u32[]{:S(2)}) %all-to-all-start.1) | async-done | bytes 4194336 | tf_op jit(solution)/shard_map/all_to_all | solution.py:105
  168.3 5.6 %all-to-all-start.2 = ((bf16[16,256,2,256]{3,1,2,0:T(8,128)(2,1)}), bf16[16,256,2,256]{3,1,2,0:T(8,128)(2,1)}, u32[]{:S(2)}, u32[]{:S(2)}) async-start(bf16[16,256,2,256]{3,1,2,0:T(8,128)(2,1)} %copy.84), calls=%async_computation.2 | async-start | bytes 8388608 | tf_op jit(solution)/shard_map/all_to_all | solution.py:105
  176.3 2.1 fusion.52
  178.3 2.6 fusion.53
  181.0 2.8 %convert_reduce_fusion.1 = f32[256,2,256]{2,0,1:T(8,128)S(1)} fusion(bf16[16,256,2,256]{3,1,2,0:T(8,128)(2,1)} %all-to-all-done.1), kind=kLoop, calls=%fused_computation.6 | loop fusion | flops 4063232 | bytes 4718592 | tf_op jit(solution)/shard_map/reduce_sum | solution.py:106
  184.2 39.0 %all-to-all-done.2 = bf16[16,256,2,256]{3,1,2,0:T(8,128)(2,1)} async-done(((bf16[16,256,2,256]{3,1,2,0:T(8,128)(2,1)}), bf16[16,256,2,256]{3,1,2,0:T(8,128)(2,1)}, u32[]{:S(2)}, u32[]{:S(2)}) %all-to-all-start.2) | async-done | bytes 4194336 | tf_op jit(solution)/shard_map/all_to_all | solution.py:105
  223.2 2.8 %convert_reduce_fusion = f32[256,2,256]{2,0,1:T(8,128)S(1)} fusion(bf16[16,256,2,256]{3,1,2,0:T(8,128)(2,1)} %all-to-all-done.2), kind=kLoop, calls=%fused_computation.4 | loop fusion | flops 4063232 | bytes 4718592 | tf_op jit(solution)/shard_map/reduce_sum | solution.py:106
  226.4 1.8 maximum_bitcast_fusion
  228.3 8.2 %all-to-all-start.3 = ((f32[16,2,2,16,256]{4,2,3,1,0:T(2,128)}), f32[16,2,2,16,256]{4,2,3,1,0:T(2,128)S(1)}, u32[]{:S(2)}, u32[]{:S(2)}) async-start(f32[16,2,2,16,256]{4,2,3,1,0:T(2,128)} %maximum_bitcast_fusion), calls=%async_computation.3 | async-start | bytes 2097152 | tf_op jit(solution)/shard_map/all_to_all | solution.py:118
  238.5 3.6 %convolution_bitcast_fusion.2 = f32[256,4096]{1,0:T(8,128)S(1)} fusion(bf16[2,256,256]{2,1,0:T(8,128)(2,1)S(1)} %copy-done.8, bf16[2,2,256,4096]{3,2,1,0:T(8,128)(2,1)} %all-gather.2.cloned.1.call-done), kind=kOutput, calls=%fused_computation.10 | convolution fusion | flops 1073741824 | bytes 8650752 | tf_op jit(solution)/shard_map/ekd,ekc->dc/dot_general | solution.py:89
  242.0 3.6 %fusion.8 = bf16[1,4096,256]{1,2,0:T(8,128)(2,1)S(1)} fusion(f32[256,4096]{1,0:T(8,128)S(1)} %convolution_bitcast_fusion.2, bf16[2,256,256]{2,1,0:T(8,128)(2,1)S(1)} %copy-done.10, bf16[2,2,256,4096]{3,2,1,0:T(8,128)(2,1)} %all-gather.2.cloned.1.call-done), kind=kOutput, calls=%fused_computation.16 | convolution fusion | flops 1075838976 | bytes 10747904 | tf_op jit(solution)/shard_map/ekd,ekc->dc/dot_general | solution.py:89
  245.7 2.5 copy.90
  248.1 3.5 %convolution_bitcast_fusion = f32[256,4096]{1,0:T(8,128)S(1)} fusion(bf16[2,2,256,4096]{3,2,1,0:T(8,128)(2,1)} %all-gather.2.cloned.1.call-done, bf16[2,256,256]{2,1,0:T(8,128)(2,1)S(1)} %convolution_convert_fusion), kind=kOutput, calls=%fused_computation.8 | convolution fusion | flops 1073741824 | bytes 8650752 | tf_op jit(solution)/shard_map/ekd,ekc->dc/dot_general | solution.py:92
  251.6 5.1 %fusion.9 = bf16[1,4096,256]{1,2,0:T(8,128)(2,1)} fusion(f32[256,4096]{1,0:T(8,128)S(1)} %convolution_bitcast_fusion, bf16[2,2,256,4096]{3,2,1,0:T(8,128)(2,1)} %all-gather.2.cloned.1.call-done, bf16[2,256,256]{2,1,0:T(8,128)(2,1)S(1)} %copy-done.6), kind=kOutput, calls=%fused_computation.17 | convolution fusion | flops 1075838976 | bytes 10747904 | tf_op jit(solution)/shard_map/ekd,ekc->dc/dot_general | solution.py:92
  256.7 4.1 %copy.91 = bf16[1,4096,256]{2,1,0:T(8,128)(2,1)} copy(bf16[1,4096,256]{1,2,0:T(8,128)(2,1)} %fusion.9) | data formatting | bytes 4194304
  260.8 6.4 %all-to-all-done.3 = f32[16,2,2,16,256]{4,2,3,1,0:T(2,128)S(1)} async-done(((f32[16,2,2,16,256]{4,2,3,1,0:T(2,128)}), f32[16,2,2,16,256]{4,2,3,1,0:T(2,128)S(1)}, u32[]{:S(2)}, u32[]{:S(2)}) %all-to-all-start.3) | async-done | bytes 1048608 | tf_op jit(solution)/shard_map/all_to_all | solution.py:118
  (63 shorter events, 16.3 us)
Async XLA Ops:
  7.2 95.6 %copy-start = (bf16[1,4096,256]{2,1,0:T(8,128)(2,1)S(1)}, bf16[1,4096,256]{2,1,0:T(8,128)(2,1)}, u32[]{:S(2)}) copy-start(bf16[1,4096,256]{2,1,0:T(8,128)(2,1)} %param.12) | copy-start | bytes 6291460
  7.2 90.2 %all-gather.2.cloned.1.call-start = ((), (), s32[]{:S(2)}) async-start(), calls=%async_computation.4 | async-start | bytes 8912896 | tf_op jit(solution)/shard_map/all_gather | solution.py:68
  38.3 63.4 %copy-start.11 = (bf16[1,2,2,256,256]{4,3,2,1,0:T(8,128)(2,1)S(1)}, bf16[1,2,2,256,256]{4,3,2,1,0:T(8,128)(2,1)}, u32[]{:S(2)}) copy-start(bf16[1,2,2,256,256]{4,3,2,1,0:T(8,128)(2,1)} %param.11) | copy-start | bytes 1572868
  97.4 5.4 %copy-start.2 = (bf16[2,2,256,4096]{3,2,1,0:T(8,128)(2,1)S(1)}, bf16[2,2,256,4096]{3,2,1,0:T(8,128)(2,1)}, u32[]{:S(2)}) copy-start(bf16[2,2,256,4096]{3,2,1,0:T(8,128)(2,1)} %all-gather.2.cloned.1.call-done) | copy-start | bytes 25165828
  101.6 2.5 copy-start.12
  102.8 1.3 copy-start.14
  104.1 6.2 %copy-start.16 = (bf16[2,256,256]{2,1,0:T(8,128)(2,1)}, bf16[2,256,256]{2,1,0:T(8,128)(2,1)S(1)}, u32[]{:S(2)}) copy-start(bf16[2,256,256]{2,1,0:T(8,128)(2,1)S(1)} %fusion.45) | copy-start | bytes 786436
  106.9 3.4 %copy-start.5 = (bf16[2,256,256]{2,1,0:T(8,128)(2,1)}, bf16[2,256,256]{2,1,0:T(8,128)(2,1)S(1)}, u32[]{:S(2)}) copy-start(bf16[2,256,256]{2,1,0:T(8,128)(2,1)S(1)} %convolution_convert_fusion.1) | copy-start | bytes 786436
  108.9 1.3 copy-start.9
  109.0 1.7 copy-start.3
  114.2 54.2 %all-to-all-start.1 = ((bf16[16,256,2,256]{3,1,2,0:T(8,128)(2,1)}), bf16[16,256,2,256]{3,1,2,0:T(8,128)(2,1)}, u32[]{:S(2)}, u32[]{:S(2)}) async-start(bf16[16,256,2,256]{3,1,2,0:T(8,128)(2,1)} %copy.81), calls=%async_computation.1 | async-start | bytes 8388608 | tf_op jit(solution)/shard_map/all_to_all | solution.py:105
  127.8 2.2 copy-start.18
  132.0 3.1 %copy-start.7 = (bf16[2,256,256]{2,1,0:T(8,128)(2,1)}, bf16[2,256,256]{2,1,0:T(8,128)(2,1)S(1)}, u32[]{:S(2)}) copy-start(bf16[2,256,256]{2,1,0:T(8,128)(2,1)S(1)} %convolution_convert_fusion.2) | copy-start | bytes 786436
  133.8 1.6 copy-start.4
  138.9 35.0 %copy-start.13 = (bf16[2,256,256]{2,1,0:T(8,128)(2,1)S(1)}, bf16[2,256,256]{2,1,0:T(8,128)(2,1)}, u32[]{:S(2)}) copy-start(bf16[2,256,256]{2,1,0:T(8,128)(2,1)} %copy-done.12) | copy-start | bytes 786436
  139.0 35.0 %copy-start.15 = (bf16[1,2,2,256,256]{4,3,2,1,0:T(8,128)(2,1)S(1)}, bf16[1,2,2,256,256]{4,3,2,1,0:T(8,128)(2,1)}, u32[]{:S(2)}) copy-start(bf16[1,2,2,256,256]{4,3,2,1,0:T(8,128)(2,1)} %param.10) | copy-start | bytes 1572868
  139.0 35.0 %copy-start.17 = (bf16[2,256,256]{2,1,0:T(8,128)(2,1)S(1)}, bf16[2,256,256]{2,1,0:T(8,128)(2,1)}, u32[]{:S(2)}) copy-start(bf16[2,256,256]{2,1,0:T(8,128)(2,1)} %copy-done.16) | copy-start | bytes 786436
  139.0 35.6 %copy-start.19 = (bf16[2,256,256]{2,1,0:T(8,128)(2,1)S(1)}, bf16[2,256,256]{2,1,0:T(8,128)(2,1)}, u32[]{:S(2)}) copy-start(bf16[2,256,256]{2,1,0:T(8,128)(2,1)} %copy-done.18) | copy-start | bytes 786436
  168.3 54.8 %all-to-all-start.2 = ((bf16[16,256,2,256]{3,1,2,0:T(8,128)(2,1)}), bf16[16,256,2,256]{3,1,2,0:T(8,128)(2,1)}, u32[]{:S(2)}, u32[]{:S(2)}) async-start(bf16[16,256,2,256]{3,1,2,0:T(8,128)(2,1)} %copy.84), calls=%async_computation.2 | async-start | bytes 8388608 | tf_op jit(solution)/shard_map/all_to_all | solution.py:105
  226.0 12.4 %copy-start.8 = (bf16[2,256,256]{2,1,0:T(8,128)(2,1)S(1)}, bf16[2,256,256]{2,1,0:T(8,128)(2,1)}, u32[]{:S(2)}) copy-start(bf16[2,256,256]{2,1,0:T(8,128)(2,1)} %copy-done.7) | copy-start | bytes 786436
  228.3 38.9 %all-to-all-start.3 = ((f32[16,2,2,16,256]{4,2,3,1,0:T(2,128)}), f32[16,2,2,16,256]{4,2,3,1,0:T(2,128)S(1)}, u32[]{:S(2)}, u32[]{:S(2)}) async-start(f32[16,2,2,16,256]{4,2,3,1,0:T(2,128)} %maximum_bitcast_fusion), calls=%async_computation.3 | async-start | bytes 2097152 | tf_op jit(solution)/shard_map/all_to_all | solution.py:118
  238.5 3.6 %copy-start.10 = (bf16[2,256,256]{2,1,0:T(8,128)(2,1)S(1)}, bf16[2,256,256]{2,1,0:T(8,128)(2,1)}, u32[]{:S(2)}) copy-start(bf16[2,256,256]{2,1,0:T(8,128)(2,1)} %copy-done.9) | copy-start | bytes 786436
  248.1 3.5 %copy-start.6 = (bf16[2,256,256]{2,1,0:T(8,128)(2,1)S(1)}, bf16[2,256,256]{2,1,0:T(8,128)(2,1)}, u32[]{:S(2)}) copy-start(bf16[2,256,256]{2,1,0:T(8,128)(2,1)} %copy-done.5) | copy-start | bytes 786436
  251.6 16.6 %copy-start.1 = (bf16[1,4096,256]{2,1,0:T(8,128)(2,1)S(1)}, bf16[1,4096,256]{2,1,0:T(8,128)(2,1)}, u32[]{:S(2)}) copy-start(bf16[1,4096,256]{2,1,0:T(8,128)(2,1)} %param.12) | copy-start | bytes 6291460
Sparse Core Ops, SparseCore 0:
  36.7 60.6 all-gather.1
